TPU v7x, 32 devices: a whole 2x2x4 slice. The times are simulated.
32 devices in a mesh: freq: 4 (over z), blk: 8 (over y, x, core).
Axes of the slice: x: 2, y: 2, z: 4, core: 2. Of those that a mesh axis runs over, the one named last changes fastest.
Arguments:
- spectra: bfloat16 [8, 512, 2, 32, 128], P('blk', 'freq'), may hold values from -6 to 6
- pair_offsets: int32 [8, 5], P('blk'), may hold values from 0 to 4, as said below
- pair_count: int32 [8], P('blk'), may hold values from 1 to 5, as said below
Outputs:
- correlations: bfloat16 [8, 5, 128, 256, 128], P('blk', None, 'freq')
Inputs may be any that keep to these rules, and one draw needn't show every extreme that they name: `pair_offsets`: for every block, slot 0 holds 0 (the block with itself) and slots 1 to 4 hold the offsets 1 to 4, each once, in an order drawn for each block. `pair_count`: slots at or beyond a block's count are unused; block 0 lists every slot.
All inputs are finite; a program needn't handle non-finite values.
Results may differ from a plain program's by a relative error of at most 0.0052.
Values may be sent and summed in bfloat16 or wider, within the bound.
No kernel may reach another device: no remote copies, remote signals or barrier semaphores. Data moves between devices by JAX's collectives and lax.ppermute only.
A program may use at most 192 MiB of HBM per device.

v0:
```python
import math

import jax
import jax.numpy as jnp
from jax import lax
from jax.sharding import PartitionSpec as P

F = 512
LAGS = 256
REACH = 4
SLOTS = 5


def from_behind(shard, axis, by):
    size = lax.axis_size(axis)
    return lax.ppermute(shard, axis, [(i, (i + by) % size) for i in range(size)])


def lag_table():
    shifted = jnp.arange(LAGS, dtype=jnp.int32) - LAGS // 2
    bins = jnp.arange(F, dtype=jnp.int32) + 1
    phase = jnp.mod(shifted[:, None] * bins[None, :], 2 * F).astype(jnp.float32) * (jnp.pi / F)
    return jnp.stack([jnp.cos(phase), -jnp.sin(phase)], axis=-1).astype(jnp.bfloat16)


def cross_spectrum(home_spec, partner):
    freq_count, parts_count, windows, stations = home_spec.shape
    row_matrix = home_spec.reshape(freq_count, 2 * windows, stations)
    real_part = partner[:, 0]
    imag_part = partner[:, 1]
    real_rows = jnp.concatenate([real_part, imag_part], axis=1)
    imag_rows = jnp.concatenate([imag_part, -real_part], axis=1)
    column_matrix = jnp.concatenate([real_rows, imag_rows], axis=2)
    summed = jnp.einsum(
        "fks,fkt->fst", row_matrix, column_matrix, preferred_element_type=jnp.float32
    )
    return summed / windows


def local(spectra, pair_offsets, pair_count):
    home_spec = spectra[0]
    fetched = [home_spec]
    for offset_step in range(1, REACH + 1):
        fetched.append(from_behind(home_spec, "blk", -offset_step))
    nearby = jnp.stack(fetched)
    partner_offsets = pair_offsets[0]
    listed = pair_count[0]

    def slot_cross(slot_index):
        partner = lax.dynamic_index_in_dim(nearby, partner_offsets[slot_index], 0, keepdims=False)
        cross_term = cross_spectrum(home_spec, partner)
        return jnp.where(slot_index < listed, cross_term, 0.0).astype(jnp.bfloat16)

    crosses = jnp.stack([slot_cross(slot_index) for slot_index in range(SLOTS)])
    lag_weights = lag_table()
    grouped = lax.all_to_all(crosses, "freq", split_axis=2, concat_axis=1, tiled=True)
    count_slots, freq_total, stations_part, double_width = grouped.shape
    regrouped = grouped.reshape(count_slots, freq_total, stations_part, 2, double_width // 2)
    lagged = jnp.einsum(
        "lfr,nfsrt->nslt", lag_weights, regrouped, preferred_element_type=jnp.float32
    )
    result = (lagged * math.sqrt(2.0 / freq_total)).astype(jnp.bfloat16)
    return result[None]


def solution(mesh):
    placed = (P("blk", "freq", None, None, None), P("blk", None), P("blk"))
    return jax.shard_map(
        local,
        mesh=mesh,
        in_specs=placed,
        out_specs=P("blk", None, "freq", None, None),
        check_vma=False,
    )
```

profile of v0, /device:TPU:6, one launch (start us, length us, event | category | flops | bytes accessed | tf_op | source)
XLA Modules:
  0.0 1326.5 jit_solution(1731177960773644525)
XLA Ops:
  0.0 0.0 collective-permute-start
  0.0 1.4 collective-permute-start.1
  1.4 0.0 collective-permute-start.2
  1.4 1.5 collective-permute-start.3
  2.9 1.5 fusion.53
  14.5 3.3 constant_dynamic-update-slice_fusion
  17.9 28.4 %collective-permute-done = bf16[128,2,32,128]{3,2,1,0:T(8,128)(2,1)} collective-permute-done((bf16[128,2,32,128]{3,2,1,0:T(8,128)(2,1)}, bf16[128,2,32,128]{3,2,1,0:T(8,128)(2,1)}, u32[]{:S(2)}, u32[]{:S(2)}) %collective-permute-start) | collective-permute-done | bytes 2097184 | tf_op jit(solution)/shard_map/ppermute | solution.py:16
  46.3 3.3 bitcast_dynamic-update-slice_fusion.8
  49.6 44.5 %collective-permute-done.1 = bf16[128,2,32,128]{3,2,1,0:T(8,128)(2,1)} collective-permute-done((bf16[128,2,32,128]{3,2,1,0:T(8,128)(2,1)}, bf16[128,2,32,128]{3,2,1,0:T(8,128)(2,1)}, u32[]{:S(2)}, u32[]{:S(2)}) %collective-permute-start.1) | collective-permute-done | bytes 2097184 | tf_op jit(solution)/shard_map/ppermute | solution.py:16
  94.1 3.3 bitcast_dynamic-update-slice_fusion.7
  97.4 39.5 %collective-permute-done.2 = bf16[128,2,32,128]{3,2,1,0:T(8,128)(2,1)} collective-permute-done((bf16[128,2,32,128]{3,2,1,0:T(8,128)(2,1)}, bf16[128,2,32,128]{3,2,1,0:T(8,128)(2,1)}, u32[]{:S(2)}, u32[]{:S(2)}) %collective-permute-start.2) | collective-permute-done | bytes 2097184 | tf_op jit(solution)/shard_map/ppermute | solution.py:16
  137.0 3.3 bitcast_dynamic-update-slice_fusion.6
  140.3 21.1 %collective-permute-done.3 = bf16[128,2,32,128]{3,2,1,0:T(8,128)(2,1)S(1)} collective-permute-done((bf16[128,2,32,128]{3,2,1,0:T(8,128)(2,1)}, bf16[128,2,32,128]{3,2,1,0:T(8,128)(2,1)S(1)}, u32[]{:S(2)}, u32[]{:S(2)}) %collective-permute-start.3) | collective-permute-done | bytes 2097184 | tf_op jit(solution)/shard_map/ppermute | solution.py:16
  161.4 1.7 bitcast_dynamic-update-slice_fusion.5
  163.2 8.0 constant_dynamic-slice_fusion
  171.1 2.4 copy_bitcast_fusion.2
  173.5 1.7 slice_bitcast_fusion.7
  175.2 0.1 fusion.49
  175.3 0.4 copy.36
  175.7 1.7 slice_bitcast_fusion.9
  177.4 0.1 fusion.48
  177.5 1.7 slice_bitcast_fusion.5
  179.2 0.1 fusion.50
  179.4 0.8 copy_bitcast_fusion
  180.2 0.0 copy-start
  180.3 1.7 slice_bitcast_fusion.3
  181.9 0.1 fusion.51
  182.1 1.7 slice_bitcast_fusion.1
  183.8 0.1 fusion.52
  183.9 0.0 copy-done
  183.9 7.0 bitcast_dynamic-update-slice_fusion.4
  190.9 0.0 copy-start.1
  191.0 6.8 bitcast_dynamic-update-slice_fusion.3
  197.8 0.0 copy-done.1
  197.8 6.9 bitcast_dynamic-update-slice_fusion.2
  204.7 0.0 copy-start.2
  204.7 0.0 copy-start.3
  204.7 6.9 bitcast_dynamic-update-slice_fusion.1
  211.6 0.0 copy-done.2
  211.6 0.0 copy-done.3
  211.6 5.4 bitcast_dynamic-update-slice_fusion
  217.0 55.5 %copy.24 = bf16[5,128,128,256]{3,1,0,2:T(8,128)(2,1)} copy(bf16[5,128,128,256]{2,3,1,0:T(8,128)(2,1)} %bitcast_dynamic-update-slice_fusion) | data formatting | bytes 83886080 | tf_op jit(solution)/shard_map/stack | solution.py:54
  272.5 11.4 all-to-all-start
  283.9 2.5 cosine_convert_fusion
  286.4 880.8 %all-to-all-done = bf16[5,128,128,256]{3,1,0,2:T(8,128)(2,1)} async-done(((bf16[5,128,128,256]{3,1,0,2:T(8,128)(2,1)}), bf16[5,128,128,256]{3,1,0,2:T(8,128)(2,1)}, u32[]{:S(2)}, u32[]{:S(2)}) %all-to-all-start) | async-done | bytes 41943072 | tf_op jit(solution)/shard_map/all_to_all | solution.py:56
  1167.2 62.7 %copy.26 = bf16[5,4,128,32,256]{2,1,4,3,0:T(4,128)(2,1)} copy(bf16[5,4,128,32,256]{4,2,0,3,1:T(8,128)(2,1)} %bitcast.43) | data formatting | bytes 83886080 | tf_op jit(solution)/shard_map/all_to_all | solution.py:56
  1229.9 60.3 %reshape.163 = bf16[5,512,32,2,128]{1,4,3,2,0:T(8,128)(2,1)} reshape(bf16[5,4,128,32,256]{2,1,4,3,0:T(4,128)(2,1)} %copy.26) | data formatting | bytes 83886080 | tf_op jit(solution)/shard_map/reshape | solution.py:58
  1290.2 22.1 %fusion.1 = bf16[1,5,32,256,128]{3,4,2,1,0:T(8,128)(2,1)} fusion(bf16[5,512,32,2,128]{1,4,3,2,0:T(8,128)(2,1)} %reshape.163, bf16[256,512,1]{1,0,2:T(8,128)(2,1)S(1)} %get-tuple-element.21, bf16[256,512,1]{1,0,2:T(8,128)(2,1)S(1)} %get-tuple-element.20), kind=kOutput, calls=%fused_computation.7 | convolution fusion | flops 10748166144 | bytes 52953088 | tf_op jit(solution)/shard_map/lfr,nfsrt->nslt/dot_general | solution.py:59
  1312.4 14.2 %copy.27 = bf16[1,5,32,256,128]{4,3,2,1,0:T(8,128)(2,1)} copy(bf16[1,5,32,256,128]{3,4,2,1,0:T(8,128)(2,1)} %fusion.1) | data formatting | bytes 20971520 | tf_op jit(solution)/shard_map/broadcast_in_dim | solution.py:63
  (2 shorter events, 0.0 us)
Async XLA Ops:
  0.0 46.3 %collective-permute-start = (bf16[128,2,32,128]{3,2,1,0:T(8,128)(2,1)}, bf16[128,2,32,128]{3,2,1,0:T(8,128)(2,1)}, u32[]{:S(2)}, u32[]{:S(2)}) collective-permute-start(bf16[128,2,32,128]{3,2,1,0:T(8,128)(2,1)} %bitcast.110), channel_id=1, source_target_pairs={{0,7},{1,0},{2,1},{3,2},{4,3},{5,4},{6,5},{7,6},{8,15},{9,8},{10,9... | collective-permute-start | bytes 6291464 | tf_op jit(solution)/shard_map/ppermute | solution.py:16
  0.0 94.1 %collective-permute-start.1 = (bf16[128,2,32,128]{3,2,1,0:T(8,128)(2,1)}, bf16[128,2,32,128]{3,2,1,0:T(8,128)(2,1)}, u32[]{:S(2)}, u32[]{:S(2)}) collective-permute-start(bf16[128,2,32,128]{3,2,1,0:T(8,128)(2,1)} %bitcast.111), channel_id=1, source_target_pairs={{0,6},{1,7},{2,0},{3,1},{4,2},{5,3},{6,4},{7,5},{8,14},{9,15},{10,... | collective-permute-start | bytes 6291464 | tf_op jit(solution)/shard_map/ppermute | solution.py:16
  1.4 135.6 %collective-permute-start.2 = (bf16[128,2,32,128]{3,2,1,0:T(8,128)(2,1)}, bf16[128,2,32,128]{3,2,1,0:T(8,128)(2,1)}, u32[]{:S(2)}, u32[]{:S(2)}) collective-permute-start(bf16[128,2,32,128]{3,2,1,0:T(8,128)(2,1)} %bitcast.112), channel_id=1, source_target_pairs={{0,5},{1,6},{2,7},{3,0},{4,1},{5,2},{6,3},{7,4},{8,13},{9,14},{10,... | collective-permute-start | bytes 6291464 | tf_op jit(solution)/shard_map/ppermute | solution.py:16
  1.4 160.0 %collective-permute-start.3 = (bf16[128,2,32,128]{3,2,1,0:T(8,128)(2,1)}, bf16[128,2,32,128]{3,2,1,0:T(8,128)(2,1)S(1)}, u32[]{:S(2)}, u32[]{:S(2)}) collective-permute-start(bf16[128,2,32,128]{3,2,1,0:T(8,128)(2,1)} %bitcast.113), channel_id=1, source_target_pairs={{0,4},{1,5},{2,6},{3,7},{4,0},{5,1},{6,2},{7,3},{8,12},{9,13},{10,... | collective-permute-start | bytes 6291464 | tf_op jit(solution)/shard_map/ppermute | solution.py:16
  180.2 3.7 copy-start
  190.9 6.8 copy-start.1
  204.7 6.9 copy-start.2
  204.7 6.9 copy-start.3
  272.5 894.7 %all-to-all-start = ((bf16[5,128,128,256]{3,1,0,2:T(8,128)(2,1)}), bf16[5,128,128,256]{3,1,0,2:T(8,128)(2,1)}, u32[]{:S(2)}, u32[]{:S(2)}) async-start(bf16[5,128,128,256]{3,1,0,2:T(8,128)(2,1)} %copy.24), calls=%async_computation | async-start | bytes 83886080 | tf_op jit(solution)/shard_map/all_to_all | solution.py:56
where the time goes:
time: 1330 us
  waiting for transfers between devices  1010 us (76%)
  local copies, waits for them, and re-layouts  229 us (17%)
  matrix products  55.2 us (4%)
  starting transfers between devices  14.4 us (1%)
    all_to_all x1, waiting for transfers between devices, local(): lax.all_to_all(crosses, 'freq', split_axis=2, concat_axis=1, tiled=True)  881 us
    ppermute x4, waiting for transfers between devices, from_behind(): lax.ppermute(shard, axis, [(i, (i + by) % size) for i in range(size)])  134 us
    all_to_all x1, local copies, waits for them, and re-layouts, local(): lax.all_to_all(crosses, 'freq', split_axis=2, concat_axis=1, tiled=True)  62.7 us
    reshape x1, local copies, waits for them, and re-layouts, local(): grouped.reshape(count_slots, freq_total, stations_part, 2, double_width /...  60.3 us
    another operation x1, local copies, waits for them, and re-layouts, local(): crosses = jnp.stack([slot_cross(slot_index) for slot_index in range(SLOTS)])  55.5 us
    dot_general x5, matrix products, cross_spectrum(): jnp.einsum('fks,fkt->fst', row_matrix, column_matrix, preferred_element_t...  33 us
  transfers between devices with their start and end apart: 5, of which 5 were waited for; matrix products, arithmetic and copies ran while one was open for 1% of the time, Pallas kernels for 0%

commit v1 on v0

v1 whole, which is shorter than its diff:
```python
import math

import jax
import jax.numpy as jnp
from jax import lax
from jax.sharding import PartitionSpec as P

F = 512
LAGS = 256
REACH = 4
SLOTS = 5


def from_behind(shard, axis, by):
    size = lax.axis_size(axis)
    return lax.ppermute(shard, axis, [(i, (i + by) % size) for i in range(size)])


def swap(shard, axis, mask):
    size = lax.axis_size(axis)
    return lax.ppermute(shard, axis, [(i, i ^ mask) for i in range(size)])


def lag_table():
    shifted = jnp.arange(LAGS, dtype=jnp.int32) - LAGS // 2
    bins = jnp.arange(F, dtype=jnp.int32) + 1
    phase = jnp.mod(shifted[:, None] * bins[None, :], 2 * F).astype(jnp.float32) * (jnp.pi / F)
    return jnp.stack([jnp.cos(phase), -jnp.sin(phase)], axis=-1).astype(jnp.bfloat16)


def cross_spectrum(home_spec, partner):
    freq_count, parts_count, windows, stations = home_spec.shape
    row_matrix = home_spec.reshape(freq_count, 2 * windows, stations)
    real_part = partner[:, 0]
    imag_part = partner[:, 1]
    real_rows = jnp.concatenate([real_part, imag_part], axis=1)
    imag_rows = jnp.concatenate([imag_part, -real_part], axis=1)
    column_matrix = jnp.concatenate([real_rows, imag_rows], axis=2)
    summed = jnp.einsum(
        "fks,fkt->fst", row_matrix, column_matrix, preferred_element_type=jnp.float32
    )
    return summed / windows


def partner_blocks(own, staged):
    if not staged:
        return [own] + [from_behind(own, "blk", -o) for o in range(1, REACH + 1)]
    b = lax.axis_index("blk")
    x_bit = (b // 2) % 2
    core = b % 2
    r4 = swap(own, "blk", 4)
    r2 = swap(jnp.where(x_bit == 1, own, r4), "blk", 2)
    r1 = swap(jnp.where(core == 1, own, r2), "blk", 1)
    r3 = swap(jnp.where(core == 1, r2, r4), "blk", 1)
    return [own, r1, r2, r3, r4]


def local(spectra, pair_offsets, pair_count, staged):
    own_part = spectra[0]
    own = lax.all_gather(own_part, "freq", axis=0, tiled=True)
    freq_total, _, _, stations = own.shape
    parts = lax.axis_size("freq")
    width = stations // parts
    q = lax.axis_index("freq")
    home = lax.dynamic_slice_in_dim(own, q * width, width, axis=3)
    partners = partner_blocks(own, staged)

    offsets = pair_offsets[0]
    listed = pair_count[0]
    lag_weights = lag_table()
    scale = math.sqrt(2.0 / freq_total)
    out = jnp.zeros((SLOTS, width, LAGS, stations), jnp.bfloat16)
    for o in range(REACH + 1):
        slot = jnp.argmax(offsets == o).astype(jnp.int32)
        cross = cross_spectrum(home, partners[o]).astype(jnp.bfloat16)
        regrouped = cross.reshape(freq_total, width, 2, stations)
        lagged = jnp.einsum(
            "lfr,fsrt->slt", lag_weights, regrouped, preferred_element_type=jnp.float32
        )
        result = (lagged * scale).astype(jnp.bfloat16)
        result = jnp.where(slot < listed, result, jnp.zeros_like(result))
        out = lax.dynamic_update_slice(out, result[None], (slot, 0, 0, 0))
    return out[None]


def solution(mesh):
    staged = mesh.shape["blk"] == 8
    placed = (P("blk", "freq", None, None, None), P("blk", None), P("blk"))
    return jax.shard_map(
        lambda s, po, pc: local(s, po, pc, staged),
        mesh=mesh,
        in_specs=placed,
        out_specs=P("blk", None, "freq", None, None),
        check_vma=False,
    )
```

time: 1330 us -> 745 us (0.56)
  the two profiles are of different devices: /device:TPU:6 before, /device:TPU:0 now
where the time goes in v1:
time: 745 us; the launch traced here: 734 us
  waiting for transfers between devices  407 us (55%)
  local copies, waits for them, and re-layouts  158 us (21%)
  matrix products  86.2 us (12%)
  other arithmetic  53.4 us (7%)
  between operations  27.2 us (4%)
    ppermute x4, waiting for transfers between devices, swap(): return lax.ppermute(shard, axis, [(i, i ^ mask) for i in range(size)])  255 us
    all_gather x1, waiting for transfers between devices, local(): own = lax.all_gather(own_part, 'freq', axis=0, tiled=True)  152 us
    reshape x5, local copies, waits for them, and re-layouts, local(): regrouped = cross.reshape(freq_total, width, 2, stations)  69.5 us
    dot_general x5, matrix products, cross_spectrum(): jnp.einsum('fks,fkt->fst', row_matrix, column_matrix, preferred_element_t...  54.7 us
    dot_general x5, matrix products, local(): jnp.einsum('lfr,fsrt->slt', lag_weights, regrouped, preferred_element_typ...  31.5 us
    squeeze x5, local copies, waits for them, and re-layouts, cross_spectrum(): real_part = partner[:, 0]  31.2 us
    neg x5, other arithmetic, cross_spectrum(): imag_rows = jnp.concatenate([imag_part, -real_part], axis=1)  26.8 us
    broadcast_in_dim x6, local copies, waits for them, and re-layouts, local(): return out[None]  19 us
  transfers between devices with their start and end apart: 5, of which 3 were waited for; matrix products, arithmetic and copies ran while one was open for 30% of the time, Pallas kernels for 0%

profile of v1, /device:TPU:0, one launch (start us, length us, event | category | flops | bytes accessed | tf_op | source)
XLA Modules:
  0.0 733.7 jit_solution(17974986806920645358)
XLA Ops:
  6.5 0.0 all-gather.3.cloned.1.call-start
  6.5 3.3 copy.15
  9.8 0.0 all-gather.3.cloned.1.call-update
  9.8 152.5 %all-gather.3.cloned.1.call-done = bf16[1,512,2,32,128]{4,3,1,2,0:T(8,128)(2,1)} async-done(((bf16[1,128,2,32,128]{4,3,1,2,0:T(8,128)(2,1)}), bf16[1,512,2,32,128]{4,3,1,2,0:T(8,128)(2,1)}) %all-gather.3.cloned.1.call-update) | async-done | bytes 8388624 | tf_op jit(solution)/shard_map/all_gather | solution.py:60
  162.3 1.5 collective-permute-start
  163.8 181.3 %collective-permute-done = bf16[512,2,32,128]{3,2,0,1:T(8,128)(2,1)} collective-permute-done((bf16[512,2,32,128]{3,2,0,1:T(8,128)(2,1)}, bf16[512,2,32,128]{3,2,0,1:T(8,128)(2,1)}, u32[]{:S(2)}, u32[]{:S(2)}) %collective-permute-start) | collective-permute-done | bytes 8388640 | tf_op jit(solution)/shard_map/ppermute | solution.py:21
  345.1 8.9 %broadcast_select_fusion = bf16[512,2,32,128]{3,2,0,1:T(8,128)(2,1)} fusion(bf16[512,2,32,128]{3,2,0,1:T(8,128)(2,1)} %collective-permute-done, pred[]{:T(512)S(6)} %eq.53, bf16[1,512,2,32,128]{4,3,1,2,0:T(8,128)(2,1)} %all-gather.3.cloned.1.call-done), kind=kLoop, calls=%fused_computation.45 | loop fusion | flops 4194304 | bytes 25165824 | tf_op jit(solution)/shard_map/jit(_where)/select_n | solution.py:52
  354.0 0.0 collective-permute-start.1
  354.0 0.0 copy-done.3
  354.0 0.7 bitcast_reduce_fusion.2
  356.1 0.7 bitcast_reduce_fusion.3
  358.0 0.7 bitcast_reduce_fusion.4
  360.1 0.6 bitcast_reduce_fusion
  361.9 0.7 bitcast_reduce_fusion.1
  370.8 2.5 cosine_convert_fusion
  373.3 9.0 %constant_dynamic-slice_fusion = bf16[1,512,2,32,32]{4,3,1,2,0:T(8,128)(2,1)} fusion(bf16[1,512,2,32,128]{4,3,1,2,0:T(8,128)(2,1)} %all-gather.3.cloned.1.call-done, s32[]{:T(128)S(6)} %select_n.130), kind=kLoop, calls=%fused_computation.95 | loop fusion | bytes 4194308 | tf_op jit(solution)/shard_map/dynamic_slice | solution.py:65
  382.3 8.3 %copy.16 = bf16[1,512,2,32,32]{1,4,3,2,0:T(8,128)(2,1)S(1)} copy(bf16[1,512,2,32,32]{4,3,1,2,0:T(8,128)(2,1)} %constant_dynamic-slice_fusion) | data formatting | bytes 4194304 | tf_op jit(solution)/shard_map/dynamic_slice | solution.py:65
  390.6 7.9 %copy.17 = bf16[512,64,32]{1,2,0:T(8,128)(2,1)} copy(bf16[512,64,32]{0,2,1:T(8,128)(2,1)S(1)} %bitcast.132) | data formatting | bytes 4194304 | tf_op jit(solution)/shard_map/reshape | solution.py:33
  398.5 4.8 fusion.63
  403.2 6.2 slice_bitcast_fusion.9
  409.4 11.5 %multiply_convert_fusion.4 = bf16[512,32,256]{2,1,0:T(8,128)(2,1)} fusion(bf16[512,64,32]{1,2,0:T(8,128)(2,1)} %copy.17, bf16[512,32,128]{2,1,0:T(8,128)(2,1)} %fusion.63, bf16[512,32,128]{2,1,0:T(8,128)(2,1)} %get-tuple-element.26, bf16[512,32,128]{2,1,0:T(8,128)(2,1)} %get-tuple-element.25), kind=kOutput, calls=%fused_computation.44 | convolution fusion | flops 612368384 | bytes 23068672 | tf_op jit(solution)/shard_map/fks,fkt->fst/dot_general | solution.py:39
  420.9 13.8 %copy.37 = bf16[512,32,256]{0,2,1:T(8,128)(2,1)} copy(bf16[512,32,256]{2,1,0:T(8,128)(2,1)} %multiply_convert_fusion.4) | data formatting | bytes 16777216 | tf_op jit(solution)/shard_map/reshape | solution.py:76
  434.7 7.1 select_bitcast_fusion.4
  441.8 3.4 copy.19
  445.2 2.6 broadcast_in_dim.21
  447.9 0.3 constant_dynamic-update-slice_fusion.4
  448.1 0.0 copy-start
  448.2 0.0 slice-start
  448.2 7.9 %fusion.67 = bf16[512,32,128]{2,1,0:T(8,128)(2,1)} fusion(bf16[512,2,32,128]{3,2,0,1:T(8,128)(2,1)} %collective-permute-done), kind=kLoop, calls=%fused_computation.106 | loop fusion | flops 2097152 | bytes 8388608 | tf_op jit(solution)/shard_map/neg | solution.py:37
  456.1 6.5 slice_bitcast_fusion.1
  462.6 0.0 copy-done
  462.6 73.3 %collective-permute-done.1 = bf16[512,2,32,128]{3,2,0,1:T(8,128)(2,1)} collective-permute-done((bf16[512,2,32,128]{3,2,0,1:T(8,128)(2,1)}, bf16[512,2,32,128]{3,2,0,1:T(8,128)(2,1)}, u32[]{:S(2)}, u32[]{:S(2)}) %collective-permute-start.1) | collective-permute-done | bytes 8388640 | tf_op jit(solution)/shard_map/ppermute | solution.py:21
  535.9 11.7 %broadcast_select_fusion.1 = (bf16[512,2,32,128]{3,2,0,1:T(8,128)(2,1)}, bf16[512,2,32,128]{3,2,0,1:T(8,128)(2,1)}) fusion(bf16[512,2,32,128]{3,2,0,1:T(8,128)(2,1)} %collective-permute-done.1, bf16[512,2,32,128]{3,2,0,1:T(8,128)(2,1)} %collective-permute-done, pred[]{:T(512)S(6)} %eq.52, bf16[1,512,2,32,128]{4,3,1,2,0:T(8,128)(2,1)S(1)} %bitcast.131), kind=kLoop, calls=%fused_computation.46 | loop fusion | flops 8388608 | bytes 41943040 | tf_op jit(solution)/shard_map/jit(_where)/select_n | solution.py:54
  547.6 0.0 collective-permute-start.3
  547.6 10.4 %multiply_convert_fusion = bf16[512,32,256]{2,1,0:T(8,128)(2,1)} fusion(bf16[512,64,32]{1,2,0:T(8,128)(2,1)} %copy.17, bf16[512,32,128]{2,1,0:T(8,128)(2,1)} %fusion.67, bf16[512,32,128]{2,1,0:T(8,128)(2,1)} %get-tuple-element.16, bf16[512,32,128]{2,1,0:T(8,128)(2,1)} %get-tuple-element.15), kind=kOutput, calls=%fused_computation.40 | convolution fusion | flops 612368384 | bytes 23068672 | tf_op jit(solution)/shard_map/fks,fkt->fst/dot_general | solution.py:39
  557.9 13.8 %copy.41 = bf16[512,32,256]{0,2,1:T(8,128)(2,1)} copy(bf16[512,32,256]{2,1,0:T(8,128)(2,1)} %multiply_convert_fusion) | data formatting | bytes 16777216 | tf_op jit(solution)/shard_map/reshape | solution.py:76
  571.8 5.8 select_bitcast_fusion
  577.6 2.9 copy.31
  580.5 0.5 collective-permute-start.2
  581.0 4.6 fusion.65
  585.6 6.2 slice_bitcast_fusion.5
  591.8 10.4 %multiply_convert_fusion.2 = bf16[512,32,256]{2,1,0:T(8,128)(2,1)} fusion(bf16[512,64,32]{1,2,0:T(8,128)(2,1)} %copy.17, bf16[512,32,128]{2,1,0:T(8,128)(2,1)} %fusion.65, bf16[512,32,128]{2,1,0:T(8,128)(2,1)} %get-tuple-element.22, bf16[512,32,128]{2,1,0:T(8,128)(2,1)} %get-tuple-element.21), kind=kOutput, calls=%fused_computation.42 | convolution fusion | flops 612368384 | bytes 23068672 | tf_op jit(solution)/shard_map/fks,fkt->fst/dot_general | solution.py:39
  602.2 14.0 %copy.39 = bf16[512,32,256]{0,2,1:T(8,128)(2,1)} copy(bf16[512,32,256]{2,1,0:T(8,128)(2,1)} %multiply_convert_fusion.2) | data formatting | bytes 16777216 | tf_op jit(solution)/shard_map/reshape | solution.py:76
  616.2 5.8 select_bitcast_fusion.2
  622.0 2.9 copy.25
  624.9 0.0 collective-permute-done.3
  624.9 4.8 fusion.66
  629.6 6.2 slice_bitcast_fusion.3
  635.8 11.5 %multiply_convert_fusion.1 = bf16[512,32,256]{2,1,0:T(8,128)(2,1)} fusion(bf16[512,64,32]{1,2,0:T(8,128)(2,1)} %copy.17, bf16[512,32,128]{2,1,0:T(8,128)(2,1)} %fusion.66, bf16[512,32,128]{2,1,0:T(8,128)(2,1)} %get-tuple-element.18, bf16[512,32,128]{2,1,0:T(8,128)(2,1)} %get-tuple-element.17), kind=kOutput, calls=%fused_computation.41 | convolution fusion | flops 612368384 | bytes 23068672 | tf_op jit(solution)/shard_map/fks,fkt->fst/dot_general | solution.py:39
  647.3 13.8 %copy.40 = bf16[512,32,256]{0,2,1:T(8,128)(2,1)} copy(bf16[512,32,256]{2,1,0:T(8,128)(2,1)} %multiply_convert_fusion.1) | data formatting | bytes 16777216 | tf_op jit(solution)/shard_map/reshape | solution.py:76
  661.1 5.8 select_bitcast_fusion.1
  666.9 2.9 copy.28
  669.7 0.0 collective-permute-done.2
  669.7 4.7 fusion.64
  674.5 6.2 slice_bitcast_fusion.7
  680.6 11.0 %multiply_convert_fusion.3 = bf16[512,32,256]{2,1,0:T(8,128)(2,1)} fusion(bf16[512,64,32]{1,2,0:T(8,128)(2,1)} %copy.17, bf16[512,32,128]{2,1,0:T(8,128)(2,1)} %fusion.64, bf16[512,32,128]{2,1,0:T(8,128)(2,1)} %get-tuple-element.24, bf16[512,32,128]{2,1,0:T(8,128)(2,1)} %get-tuple-element.23), kind=kOutput, calls=%fused_computation.43 | convolution fusion | flops 612368384 | bytes 23068672 | tf_op jit(solution)/shard_map/fks,fkt->fst/dot_general | solution.py:39
  691.6 14.0 %copy.38 = bf16[512,32,256]{0,2,1:T(8,128)(2,1)} copy(bf16[512,32,256]{2,1,0:T(8,128)(2,1)} %multiply_convert_fusion.3) | data formatting | bytes 16777216 | tf_op jit(solution)/shard_map/reshape | solution.py:76
  705.7 7.1 select_bitcast_fusion.3
  712.8 4.2 copy.22
  717.0 3.3 constant_dynamic-update-slice_fusion.3
  720.3 3.1 constant_dynamic-update-slice_fusion.2
  723.4 0.0 copy-done.2
  723.4 1.5 constant_dynamic-update-slice_fusion.1
  724.9 1.5 constant_dynamic-update-slice_fusion
  (10 shorter events, 0.0 us)
Async XLA Ops:
  6.5 155.8 %all-gather.3.cloned.1.call-start = ((), (), s32[]{:S(2)}) async-start(), calls=%async_computation | async-start | bytes 10485760 | tf_op jit(solution)/shard_map/all_gather | solution.py:60
  162.3 182.7 %collective-permute-start = (bf16[512,2,32,128]{3,2,0,1:T(8,128)(2,1)}, bf16[512,2,32,128]{3,2,0,1:T(8,128)(2,1)}, u32[]{:S(2)}, u32[]{:S(2)}) collective-permute-start(bf16[512,2,32,128]{3,2,0,1:T(8,128)(2,1)} %bitcast.127), channel_id=1, source_target_pairs={{0,4},{1,5},{2,6},{3,7},{4,0},{5,1},{6,2},{7,3},{8,12},{9,13},{10,... | collective-permute-start | bytes 25165832 | tf_op jit(solution)/shard_map/ppermute | solution.py:21
  163.8 190.2 %copy-start.3 = (s32[1,5]{1,0:T(1,128)S(1)}, s32[1,5]{1,0:T(1,128)}, u32[]{:S(2)}) copy-start(s32[1,5]{1,0:T(1,128)} %param.4) | copy-start | bytes 64
  354.0 181.9 %collective-permute-start.1 = (bf16[512,2,32,128]{3,2,0,1:T(8,128)(2,1)}, bf16[512,2,32,128]{3,2,0,1:T(8,128)(2,1)}, u32[]{:S(2)}, u32[]{:S(2)}) collective-permute-start(bf16[512,2,32,128]{3,2,0,1:T(8,128)(2,1)} %broadcast_select_fusion), channel_id=1, source_target_pairs={{0,2},{1,3},{2,0},{3,1},{4,6},{5,7},{6,4},{7,5},{8,10},{9,11},{10,... | collective-permute-start | bytes 25165832 | tf_op jit(solution)/shard_map/ppermute | solution.py:21
  448.1 14.5 %copy-start = (bf16[1,5,32,256,128]{4,3,2,1,0:T(8,128)(2,1)}, bf16[1,5,32,256,128]{4,3,2,1,0:T(8,128)(2,1)S(1)}, u32[]{:S(2)}) copy-start(bf16[1,5,32,256,128]{4,3,2,1,0:T(8,128)(2,1)S(1)} %constant_dynamic-update-slice_fusion.4) | copy-start | bytes 31457284
  448.2 87.8 %slice-start = ((s8[8388608]{0:T(1024)(128)(4,1)}), s8[4194304]{0:T(1024)(128)(4,1)S(1)}, s32[]{:S(2)}) async-start(s8[8388608]{0:T(1024)(128)(4,1)} %bitcast.130), calls=%async_computation.1 | async-start | bytes 8388608
  456.1 79.8 %slice-start.1 = ((s8[8388608]{0:T(1024)(128)(4,1)}), s8[4194304]{0:T(1024)(128)(4,1)S(1)}, s32[]{:S(2)}) async-start(s8[8388608]{0:T(1024)(128)(4,1)} %bitcast.130), calls=%async_computation.2 | async-start | bytes 8388608
  547.6 77.3 %collective-permute-start.3 = (bf16[512,2,32,128]{3,2,0,1:T(8,128)(2,1)}, bf16[512,2,32,128]{3,2,0,1:T(8,128)(2,1)}, u32[]{:S(2)}, u32[]{:S(2)}) collective-permute-start(bf16[512,2,32,128]{3,2,0,1:T(8,128)(2,1)} %get-tuple-element.19), channel_id=1, source_target_pairs={{0,1},{1,0},{2,3},{3,2},{4,5},{5,4},{6,7},{7,6},{8,9},{9,8},{10,11... | collective-permute-start | bytes 25165832 | tf_op jit(solution)/shard_map/ppermute | solution.py:21
  580.5 89.3 %collective-permute-start.2 = (bf16[512,2,32,128]{3,2,0,1:T(8,128)(2,1)}, bf16[512,2,32,128]{3,2,0,1:T(8,128)(2,1)}, u32[]{:S(2)}, u32[]{:S(2)}) collective-permute-start(bf16[512,2,32,128]{3,2,0,1:T(8,128)(2,1)} %get-tuple-element.20), channel_id=1, source_target_pairs={{0,1},{1,0},{2,3},{3,2},{4,5},{5,4},{6,7},{7,6},{8,9},{9,8},{10,11... | collective-permute-start | bytes 25165832 | tf_op jit(solution)/shard_map/ppermute | solution.py:21
  712.8 12.1 %copy-start.1 = (bf16[1,1,32,256,128]{4,3,2,1,0:T(8,128)(2,1)S(1)}, bf16[1,1,32,256,128]{4,3,2,1,0:T(8,128)(2,1)}, u32[]{:S(2)}) copy-start(bf16[1,1,32,256,128]{4,3,2,1,0:T(8,128)(2,1)} %copy.31) | copy-start | bytes 6291460
  717.0 6.4 copy-start.2
Sparse Core Ops, SparseCore 0:
  10.0 152.3 all-gather.2

commit v2 on v1

v2 whole, which is shorter than its diff:
```python
import math

import jax
import jax.numpy as jnp
import numpy as np
from jax import lax
from jax.sharding import PartitionSpec as P

F = 512
LAGS = 256
REACH = 4
SLOTS = 5
CHUNKS = 4


def from_behind(shard, axis, by):
    size = lax.axis_size(axis)
    return lax.ppermute(shard, axis, [(i, (i + by) % size) for i in range(size)])


def swap(shard, axis, mask):
    size = lax.axis_size(axis)
    return lax.ppermute(shard, axis, [(i, i ^ mask) for i in range(size)])


def lag_table(bins_order):
    shifted = jnp.arange(LAGS, dtype=jnp.int32) - LAGS // 2
    bins = jnp.asarray(bins_order, dtype=jnp.int32) + 1
    phase = jnp.mod(shifted[:, None] * bins[None, :], 2 * F).astype(jnp.float32) * (jnp.pi / F)
    return jnp.stack([jnp.cos(phase), -jnp.sin(phase)], axis=-1).astype(jnp.bfloat16)


def home_rows(home):
    real_part = home[:, 0]
    imag_part = home[:, 1]
    real_cols = jnp.concatenate([real_part, imag_part], axis=1)
    imag_cols = jnp.concatenate([-imag_part, real_part], axis=1)
    return jnp.concatenate([real_cols, imag_cols], axis=2)


def cross_spectrum(rows, partner):
    freq_count, parts_count, windows, stations = partner.shape
    width = rows.shape[2] // 2
    columns = partner.reshape(freq_count, parts_count * windows, stations)
    summed = jnp.einsum("fkS,fkt->fSt", rows, columns, preferred_element_type=jnp.float32)
    return (summed / windows).astype(jnp.bfloat16).reshape(freq_count, 2, width, stations)


def partner_blocks(own, staged):
    if not staged:
        return [own] + [from_behind(own, "blk", -o) for o in range(1, REACH + 1)]
    b = lax.axis_index("blk")
    x_bit = (b // 2) % 2
    core = b % 2
    r4 = swap(own, "blk", 4)
    r2 = swap(jnp.where(x_bit == 1, own, r4), "blk", 2)
    r1 = swap(jnp.where(core == 1, own, r2), "blk", 1)
    r3 = swap(jnp.where(core == 1, r2, r4), "blk", 1)
    return [own, r1, r2, r3, r4]


def local(spectra, pair_offsets, pair_count, staged):
    own_part = spectra[0]
    local_freqs, _, _, stations = own_part.shape
    parts = lax.axis_size("freq")
    freq_total = local_freqs * parts
    chunks = CHUNKS if local_freqs % CHUNKS == 0 else 1
    piece = local_freqs // chunks
    width = stations // parts
    q = lax.axis_index("freq")

    order = np.array(
        [qq * local_freqs + j * piece + i for j in range(chunks) for qq in range(parts) for i in range(piece)]
    )
    crosses = [[] for _ in range(REACH + 1)]
    for j in range(chunks):
        own = lax.all_gather(own_part[j * piece:(j + 1) * piece], "freq", axis=0, tiled=True)
        rows = home_rows(lax.dynamic_slice_in_dim(own, q * width, width, axis=3))
        for o, partner in enumerate(partner_blocks(own, staged)):
            crosses[o].append(cross_spectrum(rows, partner))

    offsets = pair_offsets[0]
    listed = pair_count[0]
    lag_weights = lag_table(order)
    scale = math.sqrt(2.0 / freq_total)
    out = jnp.zeros((SLOTS, width, LAGS, stations), jnp.bfloat16)
    for o in range(REACH + 1):
        slot = jnp.argmax(offsets == o).astype(jnp.int32)
        cross = jnp.concatenate(crosses[o], axis=0)
        lagged = jnp.einsum("lfr,frst->slt", lag_weights, cross, preferred_element_type=jnp.float32)
        factor = jnp.where(slot < listed, scale, 0.0).astype(jnp.float32)
        result = (lagged * factor).astype(jnp.bfloat16)
        out = lax.dynamic_update_slice(out, result[None], (slot, 0, 0, 0))
    return out[None]


def solution(mesh):
    staged = mesh.shape["blk"] == 8
    placed = (P("blk", "freq", None, None, None), P("blk", None), P("blk"))
    return jax.shard_map(
        lambda s, po, pc: local(s, po, pc, staged),
        mesh=mesh,
        in_specs=placed,
        out_specs=P("blk", None, "freq", None, None),
        check_vma=False,
    )
```

time: 745 us -> 603 us (0.81)
  waiting for transfers between devices: 407 us -> 226 us
  matrix products: 86.2 us -> 123 us
  other arithmetic: 53.4 us -> 44.2 us
  local copies, waits for them, and re-layouts: 158 us -> 166 us
    ppermute x4 -> x16, waiting for transfers between devices: 255 us -> 89 us  [swap(): return lax.ppermute(shard, axis, [(i, i ^ mask) for i in range(size)])]
    dot_general x10 -> x25, matrix products: 86.2 us -> 123 us  [the longest x20 94.3 us: cross_spectrum(): jnp.einsum('fkS,fkt->fSt', rows, columns, preferred_element_type=jnp.floa...]
    squeeze x5 -> x4, local copies, waits for them, and re-layouts: 31.2 us -> 5.41 us  [home_rows(): imag_part = home[:, 1]]
    neg x5 -> x4, other arithmetic: 26.8 us -> 2.51 us  [home_rows(): imag_cols = jnp.concatenate([-imag_part, real_part], axis=1)]
    all_gather x1 -> x4, waiting for transfers between devices: 152 us -> 135 us  [local(): lax.all_gather(own_part[j * piece:(j + 1) * piece], 'freq', axis=0, tiled...]
    reshape x6 -> x20, local copies, waits for them, and re-layouts: 77.4 us -> 90.5 us  [cross_spectrum(): (summed / windows).astype(jnp.bfloat16)]
    dynamic_slice x2 -> x8, local copies, waits for them, and re-layouts: 17.3 us -> 29 us  [local(): rows = home_rows(lax.dynamic_slice_in_dim(own, q * width, width, axis=3))]
    select_n x1 -> x4, other arithmetic: 11.7 us -> 20.2 us  [partner_blocks(): r3 = swap(jnp.where(core == 1, r2, r4), 'blk', 1)]
  transfers between devices with their start and end apart: 5 -> 20, of which waited for: 3 -> 8; matrix products, arithmetic and copies ran while one was open for 30% -> 49% of each run, Pallas kernels for 0% -> 0%
where the time goes in v2:
time: 603 us; the launch traced here: 595 us
  waiting for transfers between devices  226 us (37%)
  local copies, waits for them, and re-layouts  166 us (28%)
  matrix products  123 us (20%)
  other arithmetic  44.2 us (7%)
  between operations  26.7 us (4%)
  starting transfers between devices  8.4 us (1%)
    all_gather x4, waiting for transfers between devices, local(): lax.all_gather(own_part[j * piece:(j + 1) * piece], 'freq', axis=0, tiled...  135 us
    dot_general x20, matrix products, cross_spectrum(): jnp.einsum('fkS,fkt->fSt', rows, columns, preferred_element_type=jnp.floa...  94.3 us
    reshape x20, local copies, waits for them, and re-layouts, cross_spectrum(): (summed / windows).astype(jnp.bfloat16)  90.5 us
    ppermute x16, waiting for transfers between devices, swap(): return lax.ppermute(shard, axis, [(i, i ^ mask) for i in range(size)])  89 us
    dynamic_slice x8, local copies, waits for them, and re-layouts, local(): rows = home_rows(lax.dynamic_slice_in_dim(own, q * width, width, axis=3))  29 us
    dot_general x5, matrix products, local(): jnp.einsum('lfr,frst->slt', lag_weights, cross, preferred_element_type=jn...  29 us
    broadcast_in_dim x6, local copies, waits for them, and re-layouts, local(): return out[None]  22.8 us
    select_n x4, other arithmetic, partner_blocks(): r3 = swap(jnp.where(core == 1, r2, r4), 'blk', 1)  20.2 us
  transfers between devices with their start and end apart: 20, of which 8 were waited for; matrix products, arithmetic and copies ran while one was open for 49% of the time, Pallas kernels for 0%

profile of v2, /device:TPU:0, one launch (start us, length us, event | category | flops | bytes accessed | tf_op | source)
XLA Modules:
  0.0 594.6 jit_solution(8547411504225242604)
XLA Ops:
  30.9 27.4 %all-gather.11.cloned.1.call-done = bf16[1,128,2,32,128]{4,3,2,0,1:T(8,128)(2,1)} async-done(((bf16[1,32,2,32,128]{4,3,2,0,1:T(8,128)(2,1)}), bf16[1,128,2,32,128]{4,3,2,0,1:T(8,128)(2,1)}) %all-gather.11.cloned.1.call-update) | async-done | bytes 2097168 | tf_op jit(solution)/shard_map/all_gather | solution.py:77
  58.3 3.6 constant_dynamic-slice_fusion.2
  65.1 39.5 %all-gather.13.cloned.1.call-done = bf16[1,128,2,32,128]{4,3,2,0,1:T(8,128)(2,1)} async-done(((bf16[1,32,2,32,128]{4,3,2,0,1:T(8,128)(2,1)}), bf16[1,128,2,32,128]{4,3,2,0,1:T(8,128)(2,1)}) %all-gather.13.cloned.1.call-update) | async-done | bytes 2097168 | tf_op jit(solution)/shard_map/all_gather | solution.py:77
  108.1 4.1 copy.39
  112.2 38.6 %all-gather.15.cloned.1.call-done = bf16[1,128,2,32,128]{4,3,2,0,1:T(8,128)(2,1)} async-done(((bf16[1,32,2,32,128]{4,3,2,0,1:T(8,128)(2,1)}), bf16[1,128,2,32,128]{4,3,2,0,1:T(8,128)(2,1)}) %all-gather.15.cloned.1.call-update) | async-done | bytes 2097168 | tf_op jit(solution)/shard_map/all_gather | solution.py:77
  154.4 4.1 copy.41
  166.9 30.0 %all-gather.9.cloned.1.call-done = bf16[1,128,2,32,128]{4,3,2,0,1:T(8,128)(2,1)} async-done(((bf16[1,32,2,32,128]{4,3,2,0,1:T(8,128)(2,1)}), bf16[1,128,2,32,128]{4,3,2,0,1:T(8,128)(2,1)}) %all-gather.9.cloned.1.call-update) | async-done | bytes 2097168 | tf_op jit(solution)/shard_map/all_gather | solution.py:77
  196.9 3.6 constant_dynamic-slice_fusion.3
  207.2 4.5 multiply_convert_fusion.18
  211.7 4.5 multiply_convert_fusion.17
  223.6 4.5 copy.43
  228.2 4.5 copy.44
  232.7 4.6 copy.42
  237.3 4.5 copy.45
  243.4 5.8 fusion.55
  249.2 4.4 copy.46
  259.4 5.9 multiply_convert_fusion.2
  265.3 4.5 copy.63
  269.8 4.0 broadcast_select_fusion.2
  274.6 24.3 %collective-permute-done.6 = bf16[128,2,32,128]{3,2,1,0:T(8,128)(2,1)} collective-permute-done((bf16[128,2,32,128]{3,2,1,0:T(8,128)(2,1)}, bf16[128,2,32,128]{3,2,1,0:T(8,128)(2,1)}, u32[]{:S(2)}, u32[]{:S(2)}) %collective-permute-start.6) | collective-permute-done | bytes 2097184 | tf_op jit(solution)/shard_map/ppermute | solution.py:23
  298.9 4.3 multiply_convert_fusion.1
  303.3 4.5 copy.64
  307.8 3.9 broadcast_select_fusion.1
  312.6 31.3 %collective-permute-done.9 = bf16[128,2,32,128]{3,2,1,0:T(8,128)(2,1)} collective-permute-done((bf16[128,2,32,128]{3,2,1,0:T(8,128)(2,1)}, bf16[128,2,32,128]{3,2,1,0:T(8,128)(2,1)}, u32[]{:S(2)}, u32[]{:S(2)}) %collective-permute-start.9) | collective-permute-done | bytes 2097184 | tf_op jit(solution)/shard_map/ppermute | solution.py:23
  343.9 4.3 multiply_convert_fusion
  348.2 4.5 copy.65
  352.7 4.0 broadcast_select_fusion
  357.5 30.1 %collective-permute-done = bf16[128,2,32,128]{3,2,1,0:T(8,128)(2,1)} collective-permute-done((bf16[128,2,32,128]{3,2,1,0:T(8,128)(2,1)S(1)}, bf16[128,2,32,128]{3,2,1,0:T(8,128)(2,1)}, u32[]{:S(2)}, u32[]{:S(2)}) %collective-permute-start) | collective-permute-done | bytes 2097184 | tf_op jit(solution)/shard_map/ppermute | solution.py:23
  387.7 4.4 multiply_convert_fusion.3
  392.0 4.5 copy.62
  396.6 5.9 fusion.67
  402.5 4.2 copy.66
  409.8 5.2 broadcast_select_fusion.6
  415.6 5.5 broadcast_select_fusion.5
  421.1 4.5 multiply_convert_fusion.10
  425.6 4.4 multiply_convert_fusion.9
  430.6 4.8 broadcast_select_fusion.4
  435.4 4.3 multiply_convert_fusion.8
  439.7 4.5 copy.53
  444.3 4.6 copy.54
  448.9 4.5 copy.55
  456.6 5.5 multiply_convert_fusion.11
  462.2 4.5 copy.52
  466.7 5.9 fusion.61
  472.6 4.3 copy.56
  476.9 4.7 broadcast_select_fusion.7
  481.6 4.4 multiply_convert_fusion.6
  490.0 5.6 multiply_convert_fusion.14
  495.6 4.6 copy.48
  500.3 5.6 multiply_convert_fusion.5
  505.9 4.6 copy.59
  510.4 5.6 multiply_convert_fusion.13
  516.0 4.6 copy.49
  520.6 5.2 multiply_convert_fusion.4
  525.9 4.6 copy.60
  530.4 5.2 multiply_convert_fusion.12
  535.7 4.9 copy.50
  540.6 5.3 multiply_convert_fusion.7
  545.9 4.6 copy.57
  550.5 5.6 fusion.64
  559.3 5.2 multiply_convert_fusion.15
  564.5 4.6 copy.47
  569.1 5.8 fusion.58
  574.9 4.1 copy.51
  (162 shorter events, 77.3 us)
Async XLA Ops:
  6.5 51.8 %all-gather.11.cloned.1.call-start = ((), (), s32[]{:S(2)}) async-start(), calls=%async_computation.1 | async-start | bytes 2621440 | tf_op jit(solution)/shard_map/all_gather | solution.py:77
  9.5 2.1 copy-start.46
  9.5 18.3 %copy-start.45 = (s32[512]{0:T(512)S(1)}, s32[512]{0:T(512)}, u32[]{:S(2)}) copy-start(s32[512]{0:T(512)} %constant.141) | copy-start | bytes 6148
  9.5 95.0 %all-gather.13.cloned.1.call-start = ((), (), s32[]{:S(2)}) async-start(), calls=%async_computation.2 | async-start | bytes 2621440 | tf_op jit(solution)/shard_map/all_gather | solution.py:77
  10.3 140.5 %all-gather.15.cloned.1.call-start = ((), (), s32[]{:S(2)}) async-start(), calls=%async_computation.3 | async-start | bytes 2621440 | tf_op jit(solution)/shard_map/all_gather | solution.py:77
  11.0 185.9 %all-gather.9.cloned.1.call-start = ((), (), s32[]{:S(2)}) async-start(), calls=%async_computation | async-start | bytes 2621440 | tf_op jit(solution)/shard_map/all_gather | solution.py:77
  158.5 3.2 copy-start.6
  203.8 3.3 copy-start.16
  203.9 3.3 copy-start.36
  203.9 3.4 copy-start.40
  205.2 11.2 %copy-start.20 = (bf16[128,32,32]{1,2,0:T(8,128)(2,1)}, bf16[128,32,32]{1,2,0:T(8,128)(2,1)S(1)}, u32[]{:S(2)}) copy-start(bf16[128,32,32]{1,2,0:T(8,128)(2,1)S(1)} %get-tuple-element.23) | copy-start | bytes 786436
  205.2 11.2 %copy-start.22 = (bf16[128,32,32]{1,2,0:T(8,128)(2,1)}, bf16[128,32,32]{1,2,0:T(8,128)(2,1)S(1)}, u32[]{:S(2)}) copy-start(bf16[128,32,32]{1,2,0:T(8,128)(2,1)S(1)} %get-tuple-element.24) | copy-start | bytes 786436
  205.2 53.9 %collective-permute-start.3 = (bf16[128,2,32,128]{3,2,1,0:T(8,128)(2,1)}, bf16[128,2,32,128]{3,2,1,0:T(8,128)(2,1)}, u32[]{:S(2)}, u32[]{:S(2)}) collective-permute-start(bf16[128,2,32,128]{3,2,1,0:T(8,128)(2,1)} %bitcast.34), channel_id=1, source_target_pairs={{0,4},{1,5},{2,6},{3,7},{4,0},{5,1},{6,2},{7,3},{8,12},{9,13},{10,... | collective-permute-start | bytes 6291464 | tf_op jit(solution)/shard_map/ppermute | solution.py:23
  206.6 92.3 %collective-permute-start.6 = (bf16[128,2,32,128]{3,2,1,0:T(8,128)(2,1)}, bf16[128,2,32,128]{3,2,1,0:T(8,128)(2,1)}, u32[]{:S(2)}, u32[]{:S(2)}) collective-permute-start(bf16[128,2,32,128]{3,2,1,0:T(8,128)(2,1)} %bitcast.37), channel_id=1, source_target_pairs={{0,4},{1,5},{2,6},{3,7},{4,0},{5,1},{6,2},{7,3},{8,12},{9,13},{10,... | collective-permute-start | bytes 6291464 | tf_op jit(solution)/shard_map/ppermute | solution.py:23
  207.2 4.5 copy-start.13
  207.2 4.5 copy-start.30
  207.2 4.5 copy-start.33
  211.7 4.5 copy-start.5
  216.4 4.5 copy-start.10
  218.2 2.7 copy-start.1
  218.2 2.7 copy-start.24
  218.2 2.7 copy-start.27
  241.9 102.0 %collective-permute-start.9 = (bf16[128,2,32,128]{3,2,1,0:T(8,128)(2,1)}, bf16[128,2,32,128]{3,2,1,0:T(8,128)(2,1)}, u32[]{:S(2)}, u32[]{:S(2)}) collective-permute-start(bf16[128,2,32,128]{3,2,1,0:T(8,128)(2,1)} %bitcast.184), channel_id=1, source_target_pairs={{0,4},{1,5},{2,6},{3,7},{4,0},{5,1},{6,2},{7,3},{8,12},{9,13},{10,... | collective-permute-start | bytes 6291464 | tf_op jit(solution)/shard_map/ppermute | solution.py:23
  253.6 134.0 %collective-permute-start = (bf16[128,2,32,128]{3,2,1,0:T(8,128)(2,1)S(1)}, bf16[128,2,32,128]{3,2,1,0:T(8,128)(2,1)}, u32[]{:S(2)}, u32[]{:S(2)}) collective-permute-start(bf16[128,2,32,128]{3,2,1,0:T(8,128)(2,1)S(1)} %bitcast.183), channel_id=1, source_target_pairs={{0,4},{1,5},{2,6},{3,7},{4,0},{5,1},{6,2},{7,3},{8,12},{9,13},{10,... | collective-permute-start | bytes 6291464 | tf_op jit(solution)/shard_map/ppermute | solution.py:23
  256.9 2.2 copy-start.17
  256.9 2.2 copy-start.37
  256.9 2.5 copy-start.41
  259.0 6.3 %copy-start.7 = (bf16[1,5,32,256,128]{4,3,2,1,0:T(8,128)(2,1)}, bf16[1,5,32,256,128]{4,3,2,1,0:T(8,128)(2,1)S(1)}, u32[]{:S(2)}) copy-start(bf16[1,5,32,256,128]{4,3,2,1,0:T(8,128)(2,1)S(1)} %constant_dynamic-update-slice_fusion.4) | copy-start | bytes 31457284
  269.8 29.1 %copy-start.14 = (bf16[128,32,32]{1,2,0:T(8,128)(2,1)S(1)}, bf16[128,32,32]{1,2,0:T(8,128)(2,1)}, u32[]{:S(2)}) copy-start(bf16[128,32,32]{1,2,0:T(8,128)(2,1)} %fusion.80) | copy-start | bytes 786436
  269.8 29.1 %copy-start.31 = (bf16[128,32,32]{1,2,0:T(8,128)(2,1)S(1)}, bf16[128,32,32]{1,2,0:T(8,128)(2,1)}, u32[]{:S(2)}) copy-start(bf16[128,32,32]{1,2,0:T(8,128)(2,1)} %get-tuple-element.31) | copy-start | bytes 786436
  269.8 29.1 %copy-start.34 = (bf16[128,32,32]{1,2,0:T(8,128)(2,1)S(1)}, bf16[128,32,32]{1,2,0:T(8,128)(2,1)}, u32[]{:S(2)}) copy-start(bf16[128,32,32]{1,2,0:T(8,128)(2,1)} %get-tuple-element.32) | copy-start | bytes 786436
  273.8 136.0 %collective-permute-start.4 = (bf16[128,2,32,128]{3,2,1,0:T(8,128)(2,1)}, bf16[128,2,32,128]{3,2,1,0:T(8,128)(2,1)}, u32[]{:S(2)}, u32[]{:S(2)}) collective-permute-start(bf16[128,2,32,128]{3,2,1,0:T(8,128)(2,1)} %broadcast_select_fusion.2), channel_id=1, source_target_pairs={{0,2},{1,3},{2,0},{3,1},{4,6},{5,7},{6,4},{7,5},{8,10},{9,11},{10,... | collective-permute-start | bytes 6291464 | tf_op jit(solution)/shard_map/ppermute | solution.py:23
  307.8 36.1 %copy-start.25 = (bf16[128,32,32]{1,2,0:T(8,128)(2,1)S(1)}, bf16[128,32,32]{1,2,0:T(8,128)(2,1)}, u32[]{:S(2)}) copy-start(bf16[128,32,32]{1,2,0:T(8,128)(2,1)} %get-tuple-element.33) | copy-start | bytes 786436
  307.8 36.1 %copy-start.28 = (bf16[128,32,32]{1,2,0:T(8,128)(2,1)S(1)}, bf16[128,32,32]{1,2,0:T(8,128)(2,1)}, u32[]{:S(2)}) copy-start(bf16[128,32,32]{1,2,0:T(8,128)(2,1)} %get-tuple-element.34) | copy-start | bytes 786436
  311.7 103.8 %collective-permute-start.7 = (bf16[128,2,32,128]{3,2,1,0:T(8,128)(2,1)}, bf16[128,2,32,128]{3,2,1,0:T(8,128)(2,1)}, u32[]{:S(2)}, u32[]{:S(2)}) collective-permute-start(bf16[128,2,32,128]{3,2,1,0:T(8,128)(2,1)} %broadcast_select_fusion.1), channel_id=1, source_target_pairs={{0,2},{1,3},{2,0},{3,1},{4,6},{5,7},{6,4},{7,5},{8,10},{9,11},{10,... | collective-permute-start | bytes 6291464 | tf_op jit(solution)/shard_map/ppermute | solution.py:23
  352.7 35.0 %copy-start.11 = (bf16[128,32,32]{1,2,0:T(8,128)(2,1)S(1)}, bf16[128,32,32]{1,2,0:T(8,128)(2,1)}, u32[]{:S(2)}) copy-start(bf16[128,32,32]{1,2,0:T(8,128)(2,1)} %copy-done.10) | copy-start | bytes 786436
  352.7 35.0 %copy-start.21 = (bf16[128,32,32]{1,2,0:T(8,128)(2,1)S(1)}, bf16[128,32,32]{1,2,0:T(8,128)(2,1)}, u32[]{:S(2)}) copy-start(bf16[128,32,32]{1,2,0:T(8,128)(2,1)} %copy-done.20) | copy-start | bytes 786436
  352.7 35.0 %copy-start.23 = (bf16[128,32,32]{1,2,0:T(8,128)(2,1)S(1)}, bf16[128,32,32]{1,2,0:T(8,128)(2,1)}, u32[]{:S(2)}) copy-start(bf16[128,32,32]{1,2,0:T(8,128)(2,1)} %copy-done.22) | copy-start | bytes 786436
  356.7 73.4 %collective-permute-start.10 = (bf16[128,2,32,128]{3,2,1,0:T(8,128)(2,1)}, bf16[128,2,32,128]{3,2,1,0:T(8,128)(2,1)}, u32[]{:S(2)}, u32[]{:S(2)}) collective-permute-start(bf16[128,2,32,128]{3,2,1,0:T(8,128)(2,1)} %broadcast_select_fusion), channel_id=1, source_target_pairs={{0,2},{1,3},{2,0},{3,1},{4,6},{5,7},{6,4},{7,5},{8,10},{9,11},{10,... | collective-permute-start | bytes 6291464 | tf_op jit(solution)/shard_map/ppermute | solution.py:23
  409.8 46.8 %collective-permute-start.1 = (bf16[128,2,32,128]{3,2,1,0:T(8,128)(2,1)}, bf16[128,2,32,128]{3,2,1,0:T(8,128)(2,1)}, u32[]{:S(2)}, u32[]{:S(2)}) collective-permute-start(bf16[128,2,32,128]{3,2,1,0:T(8,128)(2,1)} %broadcast_select_fusion.3), channel_id=1, source_target_pairs={{0,2},{1,3},{2,0},{3,1},{4,6},{5,7},{6,4},{7,5},{8,10},{9,11},{10,... | collective-permute-start | bytes 6291464 | tf_op jit(solution)/shard_map/ppermute | solution.py:23
  415.0 66.5 %collective-permute-start.13 = (bf16[128,2,32,128]{3,2,1,0:T(8,128)(2,1)}, bf16[128,2,32,128]{3,2,1,0:T(8,128)(2,1)}, u32[]{:S(2)}, u32[]{:S(2)}) collective-permute-start(bf16[128,2,32,128]{3,2,1,0:T(8,128)(2,1)} %get-tuple-element.17), channel_id=1, source_target_pairs={{0,1},{1,0},{2,3},{3,2},{4,5},{5,4},{6,7},{7,6},{8,9},{9,8},{10,11... | collective-permute-start | bytes 6291464 | tf_op jit(solution)/shard_map/ppermute | solution.py:23
  415.0 6.0 %copy-start.18 = (bf16[128,32,32]{1,2,0:T(8,128)(2,1)S(1)}, bf16[128,32,32]{1,2,0:T(8,128)(2,1)}, u32[]{:S(2)}) copy-start(bf16[128,32,32]{1,2,0:T(8,128)(2,1)} %fusion.79) | copy-start | bytes 786436
  415.1 6.0 %copy-start.38 = (bf16[128,32,32]{1,2,0:T(8,128)(2,1)S(1)}, bf16[128,32,32]{1,2,0:T(8,128)(2,1)}, u32[]{:S(2)}) copy-start(bf16[128,32,32]{1,2,0:T(8,128)(2,1)} %get-tuple-element.29) | copy-start | bytes 786436
  415.1 6.0 %copy-start.42 = (bf16[128,32,32]{1,2,0:T(8,128)(2,1)S(1)}, bf16[128,32,32]{1,2,0:T(8,128)(2,1)}, u32[]{:S(2)}) copy-start(bf16[128,32,32]{1,2,0:T(8,128)(2,1)} %get-tuple-element.30) | copy-start | bytes 786436
  415.1 74.4 %collective-permute-start.5 = (bf16[128,2,32,128]{3,2,1,0:T(8,128)(2,1)}, bf16[128,2,32,128]{3,2,1,0:T(8,128)(2,1)}, u32[]{:S(2)}, u32[]{:S(2)}) collective-permute-start(bf16[128,2,32,128]{3,2,1,0:T(8,128)(2,1)} %get-tuple-element.18), channel_id=1, source_target_pairs={{0,1},{1,0},{2,3},{3,2},{4,5},{5,4},{6,7},{7,6},{8,9},{9,8},{10,11... | collective-permute-start | bytes 6291464 | tf_op jit(solution)/shard_map/ppermute | solution.py:23
  421.0 79.2 %collective-permute-start.14 = (bf16[128,2,32,128]{3,2,1,0:T(8,128)(2,1)}, bf16[128,2,32,128]{3,2,1,0:T(8,128)(2,1)}, u32[]{:S(2)}, u32[]{:S(2)}) collective-permute-start(bf16[128,2,32,128]{3,2,1,0:T(8,128)(2,1)} %get-tuple-element.19), channel_id=1, source_target_pairs={{0,1},{1,0},{2,3},{3,2},{4,5},{5,4},{6,7},{7,6},{8,9},{9,8},{10,11... | collective-permute-start | bytes 6291464 | tf_op jit(solution)/shard_map/ppermute | solution.py:23
  421.1 4.5 copy-start.15
  421.1 4.5 copy-start.32
  421.1 4.5 copy-start.35
  425.6 5.0 copy-start.2
  430.1 5.4 copy-start.26
  430.1 5.4 copy-start.29
  430.1 80.4 %collective-permute-start.8 = (bf16[128,2,32,128]{3,2,1,0:T(8,128)(2,1)}, bf16[128,2,32,128]{3,2,1,0:T(8,128)(2,1)}, u32[]{:S(2)}, u32[]{:S(2)}) collective-permute-start(bf16[128,2,32,128]{3,2,1,0:T(8,128)(2,1)} %get-tuple-element.20), channel_id=1, source_target_pairs={{0,1},{1,0},{2,3},{3,2},{4,5},{5,4},{6,7},{7,6},{8,9},{9,8},{10,11... | collective-permute-start | bytes 6291464 | tf_op jit(solution)/shard_map/ppermute | solution.py:23
  456.6 64.0 %collective-permute-start.15 = (bf16[128,2,32,128]{3,2,1,0:T(8,128)(2,1)}, bf16[128,2,32,128]{3,2,1,0:T(8,128)(2,1)}, u32[]{:S(2)}, u32[]{:S(2)}) collective-permute-start(bf16[128,2,32,128]{3,2,1,0:T(8,128)(2,1)} %get-tuple-element.21), channel_id=1, source_target_pairs={{0,1},{1,0},{2,3},{3,2},{4,5},{5,4},{6,7},{7,6},{8,9},{9,8},{10,11... | collective-permute-start | bytes 6291464 | tf_op jit(solution)/shard_map/ppermute | solution.py:23
  476.9 4.7 copy-start.19
  476.9 4.7 copy-start.39
  476.9 4.7 copy-start.43
  481.6 48.8 %collective-permute-start.11 = (bf16[128,2,32,128]{3,2,1,0:T(8,128)(2,1)}, bf16[128,2,32,128]{3,2,1,0:T(8,128)(2,1)}, u32[]{:S(2)}, u32[]{:S(2)}) collective-permute-start(bf16[128,2,32,128]{3,2,1,0:T(8,128)(2,1)} %get-tuple-element.22), channel_id=1, source_target_pairs={{0,1},{1,0},{2,3},{3,2},{4,5},{5,4},{6,7},{7,6},{8,9},{9,8},{10,11... | collective-permute-start | bytes 6291464 | tf_op jit(solution)/shard_map/ppermute | solution.py:23
  489.5 51.1 %collective-permute-start.12 = (bf16[128,2,32,128]{3,2,1,0:T(8,128)(2,1)}, bf16[128,2,32,128]{3,2,1,0:T(8,128)(2,1)}, u32[]{:S(2)}, u32[]{:S(2)}) collective-permute-start(bf16[128,2,32,128]{3,2,1,0:T(8,128)(2,1)} %get-tuple-element.15), channel_id=1, source_target_pairs={{0,1},{1,0},{2,3},{3,2},{4,5},{5,4},{6,7},{7,6},{8,9},{9,8},{10,11... | collective-permute-start | bytes 6291464 | tf_op jit(solution)/shard_map/ppermute | solution.py:23
  500.2 59.0 %collective-permute-start.2 = (bf16[128,2,32,128]{3,2,1,0:T(8,128)(2,1)}, bf16[128,2,32,128]{3,2,1,0:T(8,128)(2,1)}, u32[]{:S(2)}, u32[]{:S(2)}) collective-permute-start(bf16[128,2,32,128]{3,2,1,0:T(8,128)(2,1)} %get-tuple-element.16), channel_id=1, source_target_pairs={{0,1},{1,0},{2,3},{3,2},{4,5},{5,4},{6,7},{7,6},{8,9},{9,8},{10,11... | collective-permute-start | bytes 6291464 | tf_op jit(solution)/shard_map/ppermute | solution.py:23
  535.7 4.9 copy-start.12
  564.5 4.6 copy-start.44
  579.0 3.3 copy-start.9
  583.8 2.3 copy-start.8
  (3 other events, 5.4 us)
Sparse Core Ops, SparseCore 0:
  9.7 48.6 all-gather.10
  59.9 44.5 all-gather.12
  106.1 44.6 all-gather.14
  152.2 44.6 all-gather.8

commit v3 on v2

--- a/solution.py
+++ b/solution.py
@@ -46,19 +46,6 @@
     return (summed / windows).astype(jnp.bfloat16).reshape(freq_count, 2, width, stations)
 
 
-def partner_blocks(own, staged):
-    if not staged:
-        return [own] + [from_behind(own, "blk", -o) for o in range(1, REACH + 1)]
-    b = lax.axis_index("blk")
-    x_bit = (b // 2) % 2
-    core = b % 2
-    r4 = swap(own, "blk", 4)
-    r2 = swap(jnp.where(x_bit == 1, own, r4), "blk", 2)
-    r1 = swap(jnp.where(core == 1, own, r2), "blk", 1)
-    r3 = swap(jnp.where(core == 1, r2, r4), "blk", 1)
-    return [own, r1, r2, r3, r4]
-
-
 def local(spectra, pair_offsets, pair_count, staged):
     own_part = spectra[0]
     local_freqs, _, _, stations = own_part.shape
@@ -68,28 +55,64 @@
     piece = local_freqs // chunks
     width = stations // parts
     q = lax.axis_index("freq")
+    b = lax.axis_index("blk")
+    x_bit = (b // 2) % 2
+    core = b % 2
 
     order = np.array(
         [qq * local_freqs + j * piece + i for j in range(chunks) for qq in range(parts) for i in range(piece)]
     )
-    crosses = [[] for _ in range(REACH + 1)]
-    for j in range(chunks):
-        own = lax.all_gather(own_part[j * piece:(j + 1) * piece], "freq", axis=0, tiled=True)
-        rows = home_rows(lax.dynamic_slice_in_dim(own, q * width, width, axis=3))
-        for o, partner in enumerate(partner_blocks(own, staged)):
-            crosses[o].append(cross_spectrum(rows, partner))
+    held = {"part/%d" % j: own_part[j * piece:(j + 1) * piece] for j in range(chunks)}
+    crosses = {}
+    depth = 4 if staged else 1
+    for step in range(chunks + depth + 1):
+        made = {}
+        j = step
+        if j < chunks:
+            made["own/%d" % j] = lax.all_gather(held["part/%d" % j], "freq", axis=0, tiled=True)
+        j = step - 1
+        if 0 <= j < chunks:
+            own = held["own/%d" % j]
+            made["rows/%d" % j] = home_rows(lax.dynamic_slice_in_dim(own, q * width, width, axis=3))
+            if staged:
+                made["r4/%d" % j] = swap(own, "blk", 4)
+            else:
+                for o in range(1, REACH + 1):
+                    made["r%d/%d" % (o, j)] = from_behind(own, "blk", -o)
+        if staged:
+            j = step - 2
+            if 0 <= j < chunks:
+                made["r2/%d" % j] = swap(jnp.where(x_bit == 1, held["own/%d" % j], held["r4/%d" % j]), "blk", 2)
+            j = step - 3
+            if 0 <= j < chunks:
+                made["r1/%d" % j] = swap(jnp.where(core == 1, held["own/%d" % j], held["r2/%d" % j]), "blk", 1)
+                made["r3/%d" % j] = swap(jnp.where(core == 1, held["r2/%d" % j], held["r4/%d" % j]), "blk", 1)
+        for key in list(held):
+            name, j = key.split("/")[0], int(key.split("/")[-1])
+            if name in ("own", "r1", "r2", "r3", "r4"):
+                o = 0 if name == "own" else int(name[1])
+                if "rows/%d" % j in held and (o, j) not in crosses:
+                    made["cross%d/%d" % (o, j)] = cross_spectrum(held["rows/%d" % j], held[key])
+                    crosses[(o, j)] = True
+        keep = dict(held)
+        for j in range(chunks):
+            if step >= j:
+                keep.pop("part/%d" % j, None)
+        keep.update(made)
+        held = lax.optimization_barrier(keep)
 
     offsets = pair_offsets[0]
     listed = pair_count[0]
-    lag_weights = lag_table(order)
+    weights = lag_table(order).reshape(LAGS, freq_total * 2)
     scale = math.sqrt(2.0 / freq_total)
     out = jnp.zeros((SLOTS, width, LAGS, stations), jnp.bfloat16)
     for o in range(REACH + 1):
         slot = jnp.argmax(offsets == o).astype(jnp.int32)
-        cross = jnp.concatenate(crosses[o], axis=0)
-        lagged = jnp.einsum("lfr,frst->slt", lag_weights, cross, preferred_element_type=jnp.float32)
+        cross = jnp.concatenate([held["cross%d/%d" % (o, j)] for j in range(chunks)], axis=0)
+        cross = cross.reshape(freq_total * 2, width, stations)
+        lagged = jnp.einsum("lK,Kst->lst", weights, cross, preferred_element_type=jnp.float32)
         factor = jnp.where(slot < listed, scale, 0.0).astype(jnp.float32)
-        result = (lagged * factor).astype(jnp.bfloat16)
+        result = jnp.transpose((lagged * factor).astype(jnp.bfloat16), (1, 0, 2))
         out = lax.dynamic_update_slice(out, result[None], (slot, 0, 0, 0))
     return out[None]
 

time: 603 us -> 470 us (0.78)
  waiting for transfers between devices: 226 us -> 120 us
  matrix products: 123 us -> 92.4 us
  other arithmetic: 44.2 us -> 54.4 us
  local copies, waits for them, and re-layouts: 166 us -> 157 us
    optimization_barrier x0 -> x32, local copies, waits for them, and re-layouts: none -> 110 us  [local(): held = lax.optimization_barrier(keep)]
    reshape x20 -> x0, local copies, waits for them, and re-layouts: 90.5 us -> none  [cross_spectrum(): (summed / windows).astype(jnp.bfloat16)]
    all_gather x4, waiting for transfers between devices: 135 us -> 46.6 us  [local(): lax.all_gather(held['part/%d' % j], 'freq', axis=0, tiled=True)]
    dynamic_slice x8 -> x0, local copies, waits for them, and re-layouts: 29 us -> none  [local(): rows = home_rows(lax.dynamic_slice_in_dim(own, q * width, width, axis=3))]
    dot_general x20, matrix products: 94.3 us -> 69.3 us  [cross_spectrum(): jnp.einsum('fkS,fkt->fSt', rows, columns, preferred_element_type=jnp.floa...]
    broadcast_in_dim x6 -> x1, local copies, waits for them, and re-layouts: 22.8 us -> 2.62 us  [local(): return out[None]]
    squeeze x0 -> x8, local copies, waits for them, and re-layouts: none -> 15.4 us  [home_rows(): real_part = home[:, 0]]
    ppermute x16, waiting for transfers between devices: 89 us -> 73.8 us  [swap(): return lax.ppermute(shard, axis, [(i, i ^ mask) for i in range(size)])]
  transfers between devices with their start and end apart: 20 -> 20, of which waited for: 8 -> 7; matrix products, arithmetic and copies ran while one was open for 49% -> 43% of each run, Pallas kernels for 0% -> 0%
where the time goes in v3:
time: 470 us; the launch traced here: 463 us
  local copies, waits for them, and re-layouts  157 us (33%)
  waiting for transfers between devices  120 us (26%)
  matrix products  92.4 us (20%)
  other arithmetic  54.4 us (12%)
  between operations  27.3 us (6%)
  starting transfers between devices  11.4 us (2%)
    optimization_barrier x32, local copies, waits for them, and re-layouts, local(): held = lax.optimization_barrier(keep)  110 us
    ppermute x16, waiting for transfers between devices, swap(): return lax.ppermute(shard, axis, [(i, i ^ mask) for i in range(size)])  73.8 us
    dot_general x20, matrix products, cross_spectrum(): jnp.einsum('fkS,fkt->fSt', rows, columns, preferred_element_type=jnp.floa...  69.3 us
    all_gather x4, waiting for transfers between devices, local(): lax.all_gather(held['part/%d' % j], 'freq', axis=0, tiled=True)  46.6 us
    dot_general x5, matrix products, local(): jnp.einsum('lK,Kst->lst', weights, cross, preferred_element_type=jnp.floa...  23 us
    select_n x4, other arithmetic, local(): jnp.where(core == 1, held['r2/%d' % j], held['r4/%d' % j])  18.9 us
    squeeze x8, local copies, waits for them, and re-layouts, home_rows(): real_part = home[:, 0]  15.4 us
    select_n x4, other arithmetic, local(): jnp.where(x_bit == 1, held['own/%d' % j], held['r4/%d' % j])  12.9 us
  transfers between devices with their start and end apart: 20, of which 7 were waited for; matrix products, arithmetic and copies ran while one was open for 43% of the time, Pallas kernels for 0%

profile of v3, /device:TPU:0, one launch (start us, length us, event | category | flops | bytes accessed | tf_op | source)
XLA Modules:
  0.0 462.5 jit_solution(916261216631937860)
XLA Ops:
  11.0 46.5 %all-gather.12.cloned.1.call-done = bf16[1,128,2,32,128]{4,3,2,0,1:T(8,128)(2,1)} async-done(((bf16[1,32,2,32,128]{4,3,2,0,1:T(8,128)(2,1)}), bf16[1,128,2,32,128]{4,3,2,0,1:T(8,128)(2,1)}) %all-gather.12.cloned.1.call-update) | async-done | bytes 2097168 | tf_op jit(solution)/shard_map/all_gather | solution.py:72
  68.6 36.8 %collective-permute-done = bf16[128,2,32,128]{3,2,1,0:T(8,128)(2,1)} collective-permute-done((bf16[128,2,32,128]{3,2,1,0:T(8,128)(2,1)}, bf16[128,2,32,128]{3,2,1,0:T(8,128)(2,1)}, u32[]{:S(2)}, u32[]{:S(2)}) %collective-permute-start) | collective-permute-done | bytes 2097184 | tf_op jit(solution)/shard_map/ppermute | solution.py:23
  105.5 3.3 broadcast_select_fusion.11
  115.7 2.9 copy.58
  120.0 2.9 copy.56
  122.9 4.8 %copy.54 = bf16[128,64,64]{1,2,0:T(8,128)(2,1)} copy(bf16[128,64,64]{0,2,1:T(8,128)(2,1)S(1)} %maximum_maximum_fusion) | data formatting | bytes 2097152 | tf_op jit(solution)/shard_map/optimization_barrier | solution.py:102
  129.9 4.4 multiply_convert_fusion.18
  136.4 19.2 %collective-permute-done.1 = bf16[128,2,32,128]{3,2,1,0:T(8,128)(2,1)} collective-permute-done((bf16[128,2,32,128]{3,2,1,0:T(8,128)(2,1)}, bf16[128,2,32,128]{3,2,1,0:T(8,128)(2,1)}, u32[]{:S(2)}, u32[]{:S(2)}) %collective-permute-start.1) | collective-permute-done | bytes 2097184 | tf_op jit(solution)/shard_map/ppermute | solution.py:23
  156.6 3.3 broadcast_select_fusion.10
  160.0 5.0 %broadcast_select_fusion.6 = (bf16[128,2,32,128]{3,2,1,0:T(8,128)(2,1)}, bf16[128,2,32,128]{3,2,1,0:T(8,128)(2,1)}) fusion(bf16[128,2,32,128]{3,2,1,0:T(8,128)(2,1)} %collective-permute-done.1, bf16[128,2,32,128]{3,2,1,0:T(8,128)(2,1)} %collective-permute-done, pred[]{:T(512)S(6)} %eq.58, bf16[128,2,32,128]{3,2,1,0:T(8,128)(2,1)S(1)} %bitcast.193), kind=kLoop, calls=%fused_computation.81 | loop fusion | flops 2097152 | bytes 10485761 | tf_op jit(solution)/shard_map/jit(_where)/select_n | solution.py:89
  172.9 2.9 copy.65
  177.2 2.9 copy.63
  180.1 5.4 %copy.60 = bf16[128,64,64]{1,2,0:T(8,128)(2,1)} copy(bf16[128,64,64]{0,2,1:T(8,128)(2,1)} %maximum_maximum_fusion.1) | data formatting | bytes 2097152 | tf_op jit(solution)/shard_map/optimization_barrier | solution.py:102
  185.5 4.7 %copy.61 = bf16[128,64,64]{1,2,0:T(8,128)(2,1)} copy(bf16[128,64,64]{0,2,1:T(8,128)(2,1)S(1)} %maximum_maximum_fusion) | data formatting | bytes 2097152 | tf_op jit(solution)/shard_map/optimization_barrier | solution.py:102
  192.3 4.4 multiply_convert_fusion.15
  198.8 3.7 multiply_convert_fusion.16
  202.5 3.1 collective-permute-done.4
  205.6 7.6 %collective-permute-done.6 = bf16[128,2,32,128]{3,2,1,0:T(8,128)(2,1)} collective-permute-done((bf16[128,2,32,128]{3,2,1,0:T(8,128)(2,1)S(1)}, bf16[128,2,32,128]{3,2,1,0:T(8,128)(2,1)}, u32[]{:S(2)}, u32[]{:S(2)}) %collective-permute-start.6) | collective-permute-done | bytes 2097184 | tf_op jit(solution)/shard_map/ppermute | solution.py:23
  213.2 3.0 fusion.73
  217.6 3.1 broadcast_select_fusion.9
  221.0 4.7 %broadcast_select_fusion.4 = (bf16[128,2,32,128]{3,2,1,0:T(8,128)(2,1)}, bf16[128,2,32,128]{3,2,1,0:T(8,128)(2,1)}) fusion(bf16[128,2,32,128]{3,2,1,0:T(8,128)(2,1)} %collective-permute-done.4, bf16[128,2,32,128]{3,2,1,0:T(8,128)(2,1)} %collective-permute-done.2, pred[]{:T(512)S(6)} %eq.58, bf16[128,2,32,128]{3,2,1,0:T(8,128)(2,1)S(1)} %copy-done.3), kind=kLoop, calls=%fused_computation.79 | loop fusion | flops 2097152 | bytes 10485761 | tf_op jit(solution)/shard_map/jit(_where)/select_n | solution.py:89
  231.0 2.9 copy.74
  233.9 2.9 copy.72
  236.8 5.4 %copy.67 = bf16[128,64,64]{1,2,0:T(8,128)(2,1)} copy(bf16[128,64,64]{0,2,1:T(8,128)(2,1)} %maximum_maximum_fusion.2) | data formatting | bytes 2097152 | tf_op jit(solution)/shard_map/optimization_barrier | solution.py:102
  242.2 4.5 copy.68
  246.7 5.7 %copy.69 = bf16[128,64,64]{1,2,0:T(8,128)(2,1)} copy(bf16[128,64,64]{0,2,1:T(8,128)(2,1)} %maximum_maximum_fusion.1) | data formatting | bytes 2097152 | tf_op jit(solution)/shard_map/optimization_barrier | solution.py:102
  253.7 4.6 %multiply_convert_fusion.11 = bf16[128,64,128]{2,1,0:T(8,128)(2,1)} fusion(bf16[128,64,64]{1,2,0:T(8,128)(2,1)} %copy.68, bf16[128,64,128]{2,1,0:T(8,128)(2,1)} %bitcast.28), kind=kOutput, calls=%fused_computation.61 | convolution fusion | flops 136314880 | bytes 5242880 | tf_op jit(solution)/shard_map/fkS,fkt->fSt/dot_general | solution.py:45
  258.3 3.8 multiply_convert_fusion.13
  262.1 3.6 multiply_convert_fusion.10
  267.9 3.6 multiply_convert_fusion.12
  271.5 3.2 broadcast_select_fusion.8
  276.4 4.6 %broadcast_select_fusion.2 = (bf16[128,2,32,128]{3,2,1,0:T(8,128)(2,1)}, bf16[128,2,32,128]{3,2,1,0:T(8,128)(2,1)}) fusion(bf16[128,2,32,128]{3,2,1,0:T(8,128)(2,1)} %collective-permute-done.8, bf16[128,2,32,128]{3,2,1,0:T(8,128)(2,1)} %collective-permute-done.6, pred[]{:T(512)S(6)} %eq.58, bf16[128,2,32,128]{3,2,1,0:T(8,128)(2,1)S(1)} %copy-done), kind=kLoop, calls=%fused_computation.77 | loop fusion | flops 2097152 | bytes 10485761 | tf_op jit(solution)/shard_map/jit(_where)/select_n | solution.py:89
  283.5 3.5 copy.76
  287.0 5.5 %copy.77 = bf16[128,64,64]{1,2,0:T(8,128)(2,1)} copy(bf16[128,64,64]{0,2,1:T(8,128)(2,1)} %maximum_maximum_fusion.1) | data formatting | bytes 2097152 | tf_op jit(solution)/shard_map/optimization_barrier | solution.py:102
  292.5 4.8 %copy.78 = bf16[128,64,64]{1,2,0:T(8,128)(2,1)} copy(bf16[128,64,64]{0,2,1:T(8,128)(2,1)S(1)} %copy-done.12) | data formatting | bytes 2097152 | tf_op jit(solution)/shard_map/optimization_barrier | solution.py:102
  297.3 4.5 multiply_convert_fusion.6
  301.8 3.6 multiply_convert_fusion.8
  305.4 3.6 multiply_convert_fusion.5
  309.0 3.8 multiply_convert_fusion.9
  312.8 3.6 multiply_convert_fusion.7
  316.4 6.1 %collective-permute-done.12 = bf16[128,2,32,128]{3,2,1,0:T(8,128)(2,1)} collective-permute-done((bf16[128,2,32,128]{3,2,1,0:T(8,128)(2,1)}, bf16[128,2,32,128]{3,2,1,0:T(8,128)(2,1)}, u32[]{:S(2)}, u32[]{:S(2)}) %collective-permute-start.12) | collective-permute-done | bytes 2097184 | tf_op jit(solution)/shard_map/ppermute | solution.py:23
  322.6 4.6 broadcast_select_fusion
  340.7 3.1 cosine_convert_fusion
  343.8 3.5 copy.81
  347.3 5.5 %copy.82 = bf16[128,64,64]{1,2,0:T(8,128)(2,1)} copy(bf16[128,64,64]{0,2,1:T(8,128)(2,1)} %copy-done.13) | data formatting | bytes 2097152 | tf_op jit(solution)/shard_map/optimization_barrier | solution.py:102
  352.8 3.6 multiply_convert_fusion.2
  356.4 3.8 multiply_convert_fusion.4
  360.2 3.7 multiply_convert_fusion.3
  363.9 3.7 copy.84
  372.4 2.7 copy.86
  375.1 2.7 copy.87
  383.2 2.7 copy.90
  385.9 2.7 copy.91
  391.3 3.1 copy.93
  394.3 2.7 copy.94
  399.8 2.7 copy.96
  413.2 2.9 copy.99
  423.1 2.7 copy.105
  428.5 5.4 %bitcast_dynamic-update-slice_fusion.4 = bf16[1,5,32,256,128]{4,3,2,1,0:T(8,128)(2,1)S(1)} fusion(bf16[1,5,32,256,128]{4,3,2,1,0:T(8,128)(2,1)S(1)} %broadcast_in_dim.21, s32[]{:T(128)S(6)} %select_n.155, f32[]{:T(128)S(6)} %select_n.154, bf16[128,2,32,128]{3,0,1,2:T(8,128)(2,1)} %copy.89, bf16[128,2,32,128]{3,0,1,2:T(8,128)(2,1)} %copy.88, ...), kind=kOutput, calls=%fused_computation.74 | convolution fusion | flops 2184183808 | bytes 11010056 | tf_op jit(solution)/shard_map/lK,Kst->lst/dot_general | solution.py:113
  433.9 4.4 bitcast_dynamic-update-slice_fusion.3
  438.4 4.7 %bitcast_dynamic-update-slice_fusion.2 = bf16[1,5,32,256,128]{4,3,2,1,0:T(8,128)(2,1)S(1)} fusion(bf16[1,5,32,256,128]{4,3,2,1,0:T(8,128)(2,1)S(1)} %bitcast_dynamic-update-slice_fusion.3, s32[]{:T(128)S(6)} %select_n.159, f32[]{:T(128)S(6)} %select_n.158, bf16[128,2,32,128]{3,0,1,2:T(8,128)(2,1)} %copy.97, bf16[128,2,32,128]{3,0,1,2:T(8,128)(2,1)} %copy.96, ...), kind=kOutput, calls=%fused_computation.72 | convolution fusion | flops 2184183808 | bytes 11010056 | tf_op jit(solution)/shard_map/lK,Kst->lst/dot_general | solution.py:113
  443.2 4.7 %bitcast_dynamic-update-slice_fusion.1 = bf16[1,5,32,256,128]{4,3,2,1,0:T(8,128)(2,1)S(1)} fusion(bf16[1,5,32,256,128]{4,3,2,1,0:T(8,128)(2,1)S(1)} %bitcast_dynamic-update-slice_fusion.2, s32[]{:T(128)S(6)} %select_n.161, f32[]{:T(128)S(6)} %select_n.160, bf16[128,2,32,128]{3,0,1,2:T(8,128)(2,1)S(1)} %copy-done.45, ...), kind=kOutput, calls=%fused_computation.71 | convolution fusion | flops 2184183808 | bytes 11010056 | tf_op jit(solution)/shard_map/lK,Kst->lst/dot_general | solution.py:113
  448.0 4.1 copy-done.15
  452.0 3.8 bitcast_dynamic-update-slice_fusion
  (181 shorter events, 93.0 us)
Async XLA Ops:
  6.5 51.1 %all-gather.12.cloned.1.call-start = ((), (), s32[]{:S(2)}) async-start(), calls=%async_computation.3 | async-start | bytes 2621440 | tf_op jit(solution)/shard_map/all_gather | solution.py:72
  8.4 97.0 %all-gather.6.cloned.1.call-start = ((), (), s32[]{:S(2)}) async-start(), calls=%async_computation | async-start | bytes 2621440 | tf_op jit(solution)/shard_map/all_gather | solution.py:72
  57.6 99.0 %all-gather.8.cloned.1.call-start = ((), (), s32[]{:S(2)}) async-start(), calls=%async_computation.1 | async-start | bytes 2621440 | tf_op jit(solution)/shard_map/all_gather | solution.py:72
  57.7 47.8 %collective-permute-start = (bf16[128,2,32,128]{3,2,1,0:T(8,128)(2,1)}, bf16[128,2,32,128]{3,2,1,0:T(8,128)(2,1)}, u32[]{:S(2)}, u32[]{:S(2)}) collective-permute-start(bf16[128,2,32,128]{3,2,1,0:T(8,128)(2,1)} %bitcast.188), channel_id=1, source_target_pairs={{0,4},{1,5},{2,6},{3,7},{4,0},{5,1},{6,2},{7,3},{8,12},{9,13},{10,... | collective-permute-start | bytes 6291464 | tf_op jit(solution)/shard_map/ppermute | solution.py:23
  61.9 4.2 copy-start.4
  105.4 107.7 %all-gather.10.cloned.1.call-start = ((), (), s32[]{:S(2)}) async-start(), calls=%async_computation.2 | async-start | bytes 2621440 | tf_op jit(solution)/shard_map/all_gather | solution.py:72
  105.5 4.8 %copy-start.1 = (bf16[128,2,32,128]{3,2,1,0:T(8,128)(2,1)S(1)}, bf16[128,2,32,128]{3,2,1,0:T(8,128)(2,1)}, u32[]{:S(2)}) copy-start(bf16[128,2,32,128]{3,2,1,0:T(8,128)(2,1)} %all-gather.6.cloned.1.call-done) | copy-start | bytes 6291460
  108.8 46.8 %collective-permute-start.1 = (bf16[128,2,32,128]{3,2,1,0:T(8,128)(2,1)}, bf16[128,2,32,128]{3,2,1,0:T(8,128)(2,1)}, u32[]{:S(2)}, u32[]{:S(2)}) collective-permute-start(bf16[128,2,32,128]{3,2,1,0:T(8,128)(2,1)} %broadcast_select_fusion.11), channel_id=1, source_target_pairs={{0,2},{1,3},{2,0},{3,1},{4,6},{5,7},{6,4},{7,5},{8,10},{9,11},{10,... | collective-permute-start | bytes 6291464 | tf_op jit(solution)/shard_map/ppermute | solution.py:23
  110.3 46.3 %collective-permute-start.2 = (bf16[128,2,32,128]{3,2,1,0:T(8,128)(2,1)S(1)}, bf16[128,2,32,128]{3,2,1,0:T(8,128)(2,1)}, u32[]{:S(2)}, u32[]{:S(2)}) collective-permute-start(bf16[128,2,32,128]{3,2,1,0:T(8,128)(2,1)S(1)} %copy-done.1), channel_id=1, source_target_pairs={{0,4},{1,5},{2,6},{3,7},{4,0},{5,1},{6,2},{7,3},{8,12},{9,13},{10,... | collective-permute-start | bytes 6291464 | tf_op jit(solution)/shard_map/ppermute | solution.py:23
  129.9 4.4 copy-start.5
  129.9 4.4 copy-start.10
  156.6 3.3 copy-start.6
  160.0 5.6 %copy-start = (bf16[128,2,32,128]{3,2,1,0:T(8,128)(2,1)S(1)}, bf16[128,2,32,128]{3,2,1,0:T(8,128)(2,1)}, u32[]{:S(2)}) copy-start(bf16[128,2,32,128]{3,2,1,0:T(8,128)(2,1)} %all-gather.8.cloned.1.call-done) | copy-start | bytes 6291460
  160.0 6.9 %copy-start.50 = (s32[1,5]{1,0:T(1,128)S(1)}, s32[1,5]{1,0:T(1,128)}, u32[]{:S(2)}) copy-start(s32[1,5]{1,0:T(1,128)} %param.5) | copy-start | bytes 64
  160.0 45.6 %collective-permute-start.4 = (bf16[128,2,32,128]{3,2,1,0:T(8,128)(2,1)}, bf16[128,2,32,128]{3,2,1,0:T(8,128)(2,1)}, u32[]{:S(2)}, u32[]{:S(2)}) collective-permute-start(bf16[128,2,32,128]{3,2,1,0:T(8,128)(2,1)} %broadcast_select_fusion.10), channel_id=1, source_target_pairs={{0,2},{1,3},{2,0},{3,1},{4,6},{5,7},{6,4},{7,5},{8,10},{9,11},{10,... | collective-permute-start | bytes 6291464 | tf_op jit(solution)/shard_map/ppermute | solution.py:23
  165.0 40.6 %collective-permute-start.3 = (bf16[128,2,32,128]{3,2,1,0:T(8,128)(2,1)}, bf16[128,2,32,128]{3,2,1,0:T(8,128)(2,1)}, u32[]{:S(2)}, u32[]{:S(2)}) collective-permute-start(bf16[128,2,32,128]{3,2,1,0:T(8,128)(2,1)} %get-tuple-element.330), channel_id=1, source_target_pairs={{0,1},{1,0},{2,3},{3,2},{4,5},{5,4},{6,7},{7,6},{8,9},{9,8},{10,11... | collective-permute-start | bytes 6291464 | tf_op jit(solution)/shard_map/ppermute | solution.py:23
  165.0 40.6 %collective-permute-start.5 = (bf16[128,2,32,128]{3,2,1,0:T(8,128)(2,1)}, bf16[128,2,32,128]{3,2,1,0:T(8,128)(2,1)}, u32[]{:S(2)}, u32[]{:S(2)}) collective-permute-start(bf16[128,2,32,128]{3,2,1,0:T(8,128)(2,1)} %get-tuple-element.329), channel_id=1, source_target_pairs={{0,1},{1,0},{2,3},{3,2},{4,5},{5,4},{6,7},{7,6},{8,9},{9,8},{10,11... | collective-permute-start | bytes 6291464 | tf_op jit(solution)/shard_map/ppermute | solution.py:23
  165.5 47.6 %collective-permute-start.6 = (bf16[128,2,32,128]{3,2,1,0:T(8,128)(2,1)S(1)}, bf16[128,2,32,128]{3,2,1,0:T(8,128)(2,1)}, u32[]{:S(2)}, u32[]{:S(2)}) collective-permute-start(bf16[128,2,32,128]{3,2,1,0:T(8,128)(2,1)S(1)} %copy-done), channel_id=1, source_target_pairs={{0,4},{1,5},{2,6},{3,7},{4,0},{5,1},{6,2},{7,3},{8,12},{9,13},{10,... | collective-permute-start | bytes 6291464 | tf_op jit(solution)/shard_map/ppermute | solution.py:23
  192.3 4.4 copy-start.2
  192.3 4.4 copy-start.9
  216.2 4.8 %copy-start.3 = (bf16[128,2,32,128]{3,2,1,0:T(8,128)(2,1)S(1)}, bf16[128,2,32,128]{3,2,1,0:T(8,128)(2,1)}, u32[]{:S(2)}) copy-start(bf16[128,2,32,128]{3,2,1,0:T(8,128)(2,1)} %all-gather.6.cloned.1.call-done) | copy-start | bytes 6291460
  216.2 55.3 %collective-permute-start.10 = (bf16[128,2,32,128]{3,2,1,0:T(8,128)(2,1)}, bf16[128,2,32,128]{3,2,1,0:T(8,128)(2,1)}, u32[]{:S(2)}, u32[]{:S(2)}) collective-permute-start(bf16[128,2,32,128]{3,2,1,0:T(8,128)(2,1)} %all-gather.10.cloned.1.call-done), channel_id=1, source_target_pairs={{0,4},{1,5},{2,6},{3,7},{4,0},{5,1},{6,2},{7,3},{8,12},{9,13},{10,... | collective-permute-start | bytes 6291464 | tf_op jit(solution)/shard_map/ppermute | solution.py:23
  220.7 50.8 %collective-permute-start.8 = (bf16[128,2,32,128]{3,2,1,0:T(8,128)(2,1)}, bf16[128,2,32,128]{3,2,1,0:T(8,128)(2,1)}, u32[]{:S(2)}, u32[]{:S(2)}) collective-permute-start(bf16[128,2,32,128]{3,2,1,0:T(8,128)(2,1)} %broadcast_select_fusion.9), channel_id=1, source_target_pairs={{0,2},{1,3},{2,0},{3,1},{4,6},{5,7},{6,4},{7,5},{8,10},{9,11},{10,... | collective-permute-start | bytes 6291464 | tf_op jit(solution)/shard_map/ppermute | solution.py:23
  225.7 45.8 %collective-permute-start.7 = (bf16[128,2,32,128]{3,2,1,0:T(8,128)(2,1)}, bf16[128,2,32,128]{3,2,1,0:T(8,128)(2,1)}, u32[]{:S(2)}, u32[]{:S(2)}) collective-permute-start(bf16[128,2,32,128]{3,2,1,0:T(8,128)(2,1)} %get-tuple-element.328), channel_id=1, source_target_pairs={{0,1},{1,0},{2,3},{3,2},{4,5},{5,4},{6,7},{7,6},{8,9},{9,8},{10,11... | collective-permute-start | bytes 6291464 | tf_op jit(solution)/shard_map/ppermute | solution.py:23
  225.7 45.8 %collective-permute-start.9 = (bf16[128,2,32,128]{3,2,1,0:T(8,128)(2,1)}, bf16[128,2,32,128]{3,2,1,0:T(8,128)(2,1)}, u32[]{:S(2)}, u32[]{:S(2)}) collective-permute-start(bf16[128,2,32,128]{3,2,1,0:T(8,128)(2,1)} %get-tuple-element.327), channel_id=1, source_target_pairs={{0,1},{1,0},{2,3},{3,2},{4,5},{5,4},{6,7},{7,6},{8,9},{9,8},{10,11... | collective-permute-start | bytes 6291464 | tf_op jit(solution)/shard_map/ppermute | solution.py:23
  253.7 29.8 %copy-start.13 = (bf16[128,64,64]{0,2,1:T(8,128)(2,1)}, bf16[128,64,64]{0,2,1:T(8,128)(2,1)S(1)}, u32[]{:S(2)}) copy-start(bf16[128,64,64]{0,2,1:T(8,128)(2,1)S(1)} %maximum_maximum_fusion.3) | copy-start | bytes 3145732
  253.7 4.7 %copy-start.8 = (bf16[128,64,64]{1,2,0:T(8,128)(2,1)S(1)}, bf16[128,64,64]{1,2,0:T(8,128)(2,1)}, u32[]{:S(2)}) copy-start(bf16[128,64,64]{1,2,0:T(8,128)(2,1)} %copy.68) | copy-start | bytes 3145732
  258.3 3.8 copy-start.7
  274.7 47.9 %collective-permute-start.12 = (bf16[128,2,32,128]{3,2,1,0:T(8,128)(2,1)}, bf16[128,2,32,128]{3,2,1,0:T(8,128)(2,1)}, u32[]{:S(2)}, u32[]{:S(2)}) collective-permute-start(bf16[128,2,32,128]{3,2,1,0:T(8,128)(2,1)} %broadcast_select_fusion.8), channel_id=1, source_target_pairs={{0,2},{1,3},{2,0},{3,1},{4,6},{5,7},{6,4},{7,5},{8,10},{9,11},{10,... | collective-permute-start | bytes 6291464 | tf_op jit(solution)/shard_map/ppermute | solution.py:23
  281.0 41.6 %collective-permute-start.11 = (bf16[128,2,32,128]{3,2,1,0:T(8,128)(2,1)}, bf16[128,2,32,128]{3,2,1,0:T(8,128)(2,1)}, u32[]{:S(2)}, u32[]{:S(2)}) collective-permute-start(bf16[128,2,32,128]{3,2,1,0:T(8,128)(2,1)} %get-tuple-element.326), channel_id=1, source_target_pairs={{0,1},{1,0},{2,3},{3,2},{4,5},{5,4},{6,7},{7,6},{8,9},{9,8},{10,11... | collective-permute-start | bytes 6291464 | tf_op jit(solution)/shard_map/ppermute | solution.py:23
  281.0 41.6 %collective-permute-start.13 = (bf16[128,2,32,128]{3,2,1,0:T(8,128)(2,1)}, bf16[128,2,32,128]{3,2,1,0:T(8,128)(2,1)}, u32[]{:S(2)}, u32[]{:S(2)}) collective-permute-start(bf16[128,2,32,128]{3,2,1,0:T(8,128)(2,1)} %get-tuple-element.325), channel_id=1, source_target_pairs={{0,1},{1,0},{2,3},{3,2},{4,5},{5,4},{6,7},{7,6},{8,9},{9,8},{10,11... | collective-permute-start | bytes 6291464 | tf_op jit(solution)/shard_map/ppermute | solution.py:23
  287.0 5.5 %copy-start.12 = (bf16[128,64,64]{0,2,1:T(8,128)(2,1)S(1)}, bf16[128,64,64]{0,2,1:T(8,128)(2,1)}, u32[]{:S(2)}) copy-start(bf16[128,64,64]{0,2,1:T(8,128)(2,1)} %maximum_maximum_fusion.2) | copy-start | bytes 3145732
  297.3 4.5 copy-start.11
  309.0 3.8 copy-start.35
  322.6 18.2 %copy-start.49 = (s32[512]{0:T(512)S(1)}, s32[512]{0:T(512)}, u32[]{:S(2)}) copy-start(s32[512]{0:T(512)} %constant.123) | copy-start | bytes 6148
  327.1 36.8 %collective-permute-start.14 = (bf16[128,2,32,128]{3,2,1,0:T(8,128)(2,1)}, bf16[128,2,32,128]{3,2,1,0:T(8,128)(2,1)}, u32[]{:S(2)}, u32[]{:S(2)}) collective-permute-start(bf16[128,2,32,128]{3,2,1,0:T(8,128)(2,1)} %get-tuple-element.324), channel_id=1, source_target_pairs={{0,1},{1,0},{2,3},{3,2},{4,5},{5,4},{6,7},{7,6},{8,9},{9,8},{10,11... | collective-permute-start | bytes 6291464 | tf_op jit(solution)/shard_map/ppermute | solution.py:23
  327.1 36.8 %collective-permute-start.15 = (bf16[128,2,32,128]{3,2,1,0:T(8,128)(2,1)}, bf16[128,2,32,128]{3,2,1,0:T(8,128)(2,1)}, u32[]{:S(2)}, u32[]{:S(2)}) collective-permute-start(bf16[128,2,32,128]{3,2,1,0:T(8,128)(2,1)} %get-tuple-element.323), channel_id=1, source_target_pairs={{0,1},{1,0},{2,3},{3,2},{4,5},{5,4},{6,7},{7,6},{8,9},{9,8},{10,11... | collective-permute-start | bytes 6291464 | tf_op jit(solution)/shard_map/ppermute | solution.py:23
  356.4 3.8 copy-start.37
  360.2 3.7 copy-start.14
  372.3 2.7 copy-start.20
  375.1 2.7 copy-start.25
  380.5 2.7 copy-start.24
  383.2 2.7 copy-start.29
  385.9 2.7 copy-start.33
  391.3 3.1 copy-start.19
  394.3 2.8 copy-start.23
  397.1 2.7 copy-start.28
  399.8 2.7 copy-start.32
  402.5 2.7 copy-start.31
  407.9 2.7 copy-start.22
  413.2 2.9 copy-start.16
  417.7 2.7 copy-start.21
  420.4 2.7 copy-start.26
  428.5 5.4 %copy-start.39 = (bf16[128,2,32,128]{3,0,1,2:T(8,128)(2,1)S(1)}, bf16[128,2,32,128]{3,0,1,2:T(8,128)(2,1)}, u32[]{:S(2)}) copy-start(bf16[128,2,32,128]{3,0,1,2:T(8,128)(2,1)} %copy.90) | copy-start | bytes 6291460
  428.5 5.4 %copy-start.43 = (bf16[128,2,32,128]{3,0,1,2:T(8,128)(2,1)S(1)}, bf16[128,2,32,128]{3,0,1,2:T(8,128)(2,1)}, u32[]{:S(2)}) copy-start(bf16[128,2,32,128]{3,0,1,2:T(8,128)(2,1)} %copy.91) | copy-start | bytes 6291460
  428.5 5.4 %copy-start.47 = (bf16[128,2,32,128]{3,0,1,2:T(8,128)(2,1)S(1)}, bf16[128,2,32,128]{3,0,1,2:T(8,128)(2,1)}, u32[]{:S(2)}) copy-start(bf16[128,2,32,128]{3,0,1,2:T(8,128)(2,1)} %copy.92) | copy-start | bytes 6291460
  433.9 4.5 copy-start.40
  433.9 4.5 copy-start.44
  438.4 4.8 %copy-start.41 = (bf16[128,2,32,128]{3,0,1,2:T(8,128)(2,1)S(1)}, bf16[128,2,32,128]{3,0,1,2:T(8,128)(2,1)}, u32[]{:S(2)}) copy-start(bf16[128,2,32,128]{3,0,1,2:T(8,128)(2,1)} %copy.100) | copy-start | bytes 6291460
  438.4 4.8 %copy-start.45 = (bf16[128,2,32,128]{3,0,1,2:T(8,128)(2,1)S(1)}, bf16[128,2,32,128]{3,0,1,2:T(8,128)(2,1)}, u32[]{:S(2)}) copy-start(bf16[128,2,32,128]{3,0,1,2:T(8,128)(2,1)} %copy.101) | copy-start | bytes 6291460
  443.2 8.9 %copy-start.38 = (bf16[128,2,32,128]{3,0,1,2:T(8,128)(2,1)S(1)}, bf16[128,2,32,128]{3,0,1,2:T(8,128)(2,1)}, u32[]{:S(2)}) copy-start(bf16[128,2,32,128]{3,0,1,2:T(8,128)(2,1)} %copy.103) | copy-start | bytes 6291460
  443.2 8.9 %copy-start.42 = (bf16[128,2,32,128]{3,0,1,2:T(8,128)(2,1)S(1)}, bf16[128,2,32,128]{3,0,1,2:T(8,128)(2,1)}, u32[]{:S(2)}) copy-start(bf16[128,2,32,128]{3,0,1,2:T(8,128)(2,1)} %copy.104) | copy-start | bytes 6291460
  443.2 8.9 %copy-start.46 = (bf16[128,2,32,128]{3,0,1,2:T(8,128)(2,1)S(1)}, bf16[128,2,32,128]{3,0,1,2:T(8,128)(2,1)}, u32[]{:S(2)}) copy-start(bf16[128,2,32,128]{3,0,1,2:T(8,128)(2,1)} %copy.105) | copy-start | bytes 6291460
  447.9 4.1 copy-start.15
  (7 other events, 16.2 us)
Sparse Core Ops, SparseCore 0:
  8.9 48.6 all-gather.11
  59.2 44.6 all-gather.5
  105.6 44.8 all-gather.7
  156.7 44.2 all-gather.9

commit v4 on v3

--- a/solution.py
+++ b/solution.py
@@ -30,19 +30,19 @@
     return jnp.stack([jnp.cos(phase), -jnp.sin(phase)], axis=-1).astype(jnp.bfloat16)
 
 
-def home_rows(home):
-    real_part = home[:, 0]
-    imag_part = home[:, 1]
-    real_cols = jnp.concatenate([real_part, imag_part], axis=1)
-    imag_cols = jnp.concatenate([-imag_part, real_part], axis=1)
-    return jnp.concatenate([real_cols, imag_cols], axis=2)
+def home_rows(own, start, width):
+    freq_count, parts_count, windows, stations = own.shape
+    flat = own.reshape(freq_count, parts_count * windows, stations)
+    picked = lax.dynamic_slice_in_dim(jnp.transpose(flat, (0, 2, 1)), start, width, axis=1)
+    turned = jnp.concatenate([-picked[..., windows:], picked[..., :windows]], axis=2)
+    return jnp.concatenate([picked, turned], axis=1)
 
 
-def cross_spectrum(rows, partner):
+def cross_spectrum(rows_t, partner):
     freq_count, parts_count, windows, stations = partner.shape
-    width = rows.shape[2] // 2
+    width = rows_t.shape[1] // 2
     columns = partner.reshape(freq_count, parts_count * windows, stations)
-    summed = jnp.einsum("fkS,fkt->fSt", rows, columns, preferred_element_type=jnp.float32)
+    summed = jnp.einsum("fSk,fkt->fSt", rows_t, columns, preferred_element_type=jnp.float32)
     return (summed / windows).astype(jnp.bfloat16).reshape(freq_count, 2, width, stations)
 
 
@@ -73,7 +73,7 @@
         j = step - 1
         if 0 <= j < chunks:
             own = held["own/%d" % j]
-            made["rows/%d" % j] = home_rows(lax.dynamic_slice_in_dim(own, q * width, width, axis=3))
+            made["rows/%d" % j] = home_rows(own, q * width, width)
             if staged:
                 made["r4/%d" % j] = swap(own, "blk", 4)
             else:
@@ -88,11 +88,18 @@
                 made["r1/%d" % j] = swap(jnp.where(core == 1, held["own/%d" % j], held["r2/%d" % j]), "blk", 1)
                 made["r3/%d" % j] = swap(jnp.where(core == 1, held["r2/%d" % j], held["r4/%d" % j]), "blk", 1)
         for key in list(held):
+            if "/" not in key:
+                continue
             name, j = key.split("/")[0], int(key.split("/")[-1])
             if name in ("own", "r1", "r2", "r3", "r4"):
                 o = 0 if name == "own" else int(name[1])
                 if "rows/%d" % j in held and (o, j) not in crosses:
-                    made["cross%d/%d" % (o, j)] = cross_spectrum(held["rows/%d" % j], held[key])
+                    part = cross_spectrum(held["rows/%d" % j], held[key])
+                    name = "cross%d" % o
+                    base = made.get(name, held.get(name))
+                    if base is None:
+                        base = jnp.zeros((freq_total, 2, width, stations), jnp.bfloat16)
+                    made[name] = lax.dynamic_update_slice(base, part, (j * piece * parts, 0, 0, 0))
                     crosses[(o, j)] = True
         keep = dict(held)
         for j in range(chunks):
@@ -108,8 +115,7 @@
     out = jnp.zeros((SLOTS, width, LAGS, stations), jnp.bfloat16)
     for o in range(REACH + 1):
         slot = jnp.argmax(offsets == o).astype(jnp.int32)
-        cross = jnp.concatenate([held["cross%d/%d" % (o, j)] for j in range(chunks)], axis=0)
-        cross = cross.reshape(freq_total * 2, width, stations)
+        cross = held["cross%d" % o].reshape(freq_total * 2, width, stations)
         lagged = jnp.einsum("lK,Kst->lst", weights, cross, preferred_element_type=jnp.float32)
         factor = jnp.where(slot < listed, scale, 0.0).astype(jnp.float32)
         result = jnp.transpose((lagged * factor).astype(jnp.bfloat16), (1, 0, 2))

time: 470 us -> 398 us (0.85)
  local copies, waits for them, and re-layouts: 157 us -> 97.1 us
  matrix products: 92.4 us -> 61.6 us
  waiting for transfers between devices: 120 us -> 150 us
  other arithmetic: 54.4 us -> 45.5 us
    optimization_barrier x32 -> x0, local copies, waits for them, and re-layouts: 110 us -> none  [local(): held = lax.optimization_barrier(keep)]
    dynamic_update_slice x0 -> x19, local copies, waits for them, and re-layouts: none -> 54.9 us  [local(): lax.dynamic_update_slice(base, part, (j * piece * parts, 0, 0, 0))]
    ppermute x16, waiting for transfers between devices: 73.8 us -> 104 us  [swap(): return lax.ppermute(shard, axis, [(i, i ^ mask) for i in range(size)])]
    dot_general x20, matrix products: 69.3 us -> 39.7 us  [cross_spectrum(): jnp.einsum('fSk,fkt->fSt', rows_t, columns, preferred_element_type=jnp.fl...]
    squeeze x12 -> x0, local copies, waits for them, and re-layouts: 24.5 us -> none  [the longest x8 15.4 us: home_rows(): real_part = home[:, 0]]
    another operation x0 -> x4, local copies, waits for them, and re-layouts: none -> 13.2 us
    unnamed x102 -> x42, local copies, waits for them, and re-layouts: 4.51 us -> 15.2 us
    neg x4 -> x0, local copies, waits for them, and re-layouts: 10.5 us -> none  [home_rows(): imag_cols = jnp.concatenate([-imag_part, real_part], axis=1)]
  transfers between devices with their start and end apart: 20 -> 20, of which waited for: 7 -> 8; matrix products, arithmetic and copies ran while one was open for 43% -> 40% of each run, Pallas kernels for 0% -> 0%
where the time goes in v4:
time: 398 us; the launch traced here: 394 us
  waiting for transfers between devices  150 us (38%)
  local copies, waits for them, and re-layouts  97.1 us (24%)
  matrix products  61.6 us (15%)
  other arithmetic  45.5 us (11%)
  between operations  27.8 us (7%)
  starting transfers between devices  12 us (3%)
    ppermute x16, waiting for transfers between devices, swap(): return lax.ppermute(shard, axis, [(i, i ^ mask) for i in range(size)])  104 us
    dynamic_update_slice x19, local copies, waits for them, and re-layouts, local(): lax.dynamic_update_slice(base, part, (j * piece * parts, 0, 0, 0))  54.9 us
    all_gather x4, waiting for transfers between devices, local(): lax.all_gather(held['part/%d' % j], 'freq', axis=0, tiled=True)  46.6 us
    dot_general x20, matrix products, cross_spectrum(): jnp.einsum('fSk,fkt->fSt', rows_t, columns, preferred_element_type=jnp.fl...  39.7 us
    dot_general x5, matrix products, local(): jnp.einsum('lK,Kst->lst', weights, cross, preferred_element_type=jnp.floa...  21.9 us
    select_n x4, other arithmetic, local(): jnp.where(core == 1, held['r2/%d' % j], held['r4/%d' % j])  15.8 us
    unnamed x42, local copies, waits for them, and re-layouts  15.2 us
    another operation x4, local copies, waits for them, and re-layouts  13.2 us
  transfers between devices with their start and end apart: 20, of which 8 were waited for; matrix products, arithmetic and copies ran while one was open for 40% of the time, Pallas kernels for 0%

profile of v4, /device:TPU:0, one launch (start us, length us, event | category | flops | bytes accessed | tf_op | source)
XLA Modules:
  0.0 394.2 jit_solution(4993904172485565708)
XLA Ops:
  6.5 1.9 slice.64
  8.5 2.5 slice_bitcast_fusion
  11.0 46.6 %all-gather.12.cloned.1.call-done = bf16[1,128,2,32,128]{4,3,2,0,1:T(8,128)(2,1)} async-done(((bf16[1,32,2,32,128]{4,3,2,0,1:T(8,128)(2,1)}), bf16[1,128,2,32,128]{4,3,2,0,1:T(8,128)(2,1)}) %all-gather.12.cloned.1.call-update) | async-done | bytes 2097168 | tf_op jit(solution)/shard_map/all_gather | solution.py:72
  59.2 2.3 constant_dynamic-slice_fusion.3
  63.8 41.6 %collective-permute-done = bf16[128,2,32,128]{3,2,1,0:T(8,128)(2,1)} collective-permute-done((bf16[128,2,32,128]{3,2,1,0:T(8,128)(2,1)}, bf16[128,2,32,128]{3,2,1,0:T(8,128)(2,1)}, u32[]{:S(2)}, u32[]{:S(2)}) %collective-permute-start) | collective-permute-done | bytes 2097184 | tf_op jit(solution)/shard_map/ppermute | solution.py:23
  107.1 3.2 broadcast_select_fusion.11
  114.6 3.1 cosine_convert_fusion
  117.7 3.6 constant_dynamic-slice_fusion.2
  121.3 2.0 copy.60
  123.3 2.3 multiply_convert_fusion.18
  129.4 5.2 %dynamic_update_slice.80 = bf16[512,2,32,128]{3,0,1,2:T(8,128)(2,1)} pad(bf16[128,2,32,128]{3,0,1,2:T(8,128)(2,1)S(1)} %copy.31, bf16[]{:T(256)} %constant.102.clone.1), padding=0_384x0_0x0_0x0_0 | pad | bytes 10485762 | tf_op jit(solution)/shard_map/dynamic_update_slice | solution.py:102
  134.6 5.0 %dynamic_update_slice.81 = bf16[512,2,32,128]{3,0,1,2:T(8,128)(2,1)} pad(bf16[128,2,32,128]{3,0,1,2:T(8,128)(2,1)S(1)} %copy.32, bf16[]{:T(256)} %constant.102.clone.1), padding=0_384x0_0x0_0x0_0 | pad | bytes 10485762 | tf_op jit(solution)/shard_map/dynamic_update_slice | solution.py:102
  140.0 2.2 maximum_maximum_fusion.1
  142.2 14.9 %collective-permute-done.1 = bf16[128,2,32,128]{3,2,1,0:T(8,128)(2,1)} collective-permute-done((bf16[128,2,32,128]{3,2,1,0:T(8,128)(2,1)}, bf16[128,2,32,128]{3,2,1,0:T(8,128)(2,1)}, u32[]{:S(2)}, u32[]{:S(2)}) %collective-permute-start.1) | collective-permute-done | bytes 2097184 | tf_op jit(solution)/shard_map/ppermute | solution.py:23
  172.8 3.3 broadcast_select_fusion.10
  178.1 4.7 %broadcast_select_fusion.6 = (bf16[128,2,32,128]{3,2,1,0:T(8,128)(2,1)}, bf16[128,2,32,128]{3,2,1,0:T(8,128)(2,1)}) fusion(bf16[128,2,32,128]{3,2,1,0:T(8,128)(2,1)} %collective-permute-done.1, bf16[128,2,32,128]{3,2,1,0:T(8,128)(2,1)} %collective-permute-done, pred[]{:T(512)S(6)} %eq.58, bf16[128,2,32,128]{3,2,1,0:T(8,128)(2,1)S(1)} %bitcast.183), kind=kLoop, calls=%fused_computation.60 | loop fusion | flops 2097152 | bytes 10485761 | tf_op jit(solution)/shard_map/jit(_where)/select_n | solution.py:89
  183.4 3.6 constant_dynamic-slice_fusion.1
  187.0 2.2 copy.61
  189.2 2.3 multiply_convert_fusion.16
  192.9 5.0 %dynamic_update_slice.83 = bf16[512,2,32,128]{3,0,1,2:T(8,128)(2,1)} pad(bf16[128,2,32,128]{3,0,1,2:T(8,128)(2,1)S(1)} %copy.35, bf16[]{:T(256)} %constant.102.clone.1), padding=0_384x0_0x0_0x0_0 | pad | bytes 10485762 | tf_op jit(solution)/shard_map/dynamic_update_slice | solution.py:102
  198.4 2.2 maximum_maximum_fusion.2
  200.6 2.3 multiply_convert_fusion.15
  202.8 2.3 multiply_convert_fusion.17
  205.1 4.7 %copy_dynamic-update-slice_fusion.13 = (bf16[512,2,32,128]{3,0,1,2:T(8,128)(2,1)}, bf16[512,2,32,128]{3,0,1,2:T(8,128)(2,1)}) fusion(bf16[512,2,32,128]{3,0,1,2:T(8,128)(2,1)} %dynamic_update_slice.81, bf16[128,2,32,128]{3,2,1,0:T(8,128)(2,1)S(1)} %bitcast.219, bf16[512,2,32,128]{3,0,1,2:T(8,128)(2,1)} %dynamic_update_slice.80, ...), kind=kLoop, calls=%fused_computation.52 | loop fusion | bytes 8388608 | tf_op jit(solution)/shard_map/dynamic_update_slice | solution.py:102
  209.9 11.8 %collective-permute-done.4 = bf16[128,2,32,128]{3,2,1,0:T(8,128)(2,1)} collective-permute-done((bf16[128,2,32,128]{3,2,1,0:T(8,128)(2,1)}, bf16[128,2,32,128]{3,2,1,0:T(8,128)(2,1)}, u32[]{:S(2)}, u32[]{:S(2)}) %collective-permute-start.4) | collective-permute-done | bytes 2097184 | tf_op jit(solution)/shard_map/ppermute | solution.py:23
  223.9 3.7 constant_dynamic-slice_fusion
  227.6 2.4 copy.62
  230.0 2.3 multiply_convert_fusion.11
  233.6 2.3 multiply_convert_fusion.13
  238.7 3.2 broadcast_select_fusion.9
  243.3 4.5 %broadcast_select_fusion.4 = (bf16[128,2,32,128]{3,2,1,0:T(8,128)(2,1)}, bf16[128,2,32,128]{3,2,1,0:T(8,128)(2,1)}) fusion(bf16[128,2,32,128]{3,2,1,0:T(8,128)(2,1)} %collective-permute-done.4, bf16[128,2,32,128]{3,2,1,0:T(8,128)(2,1)} %collective-permute-done.2, pred[]{:T(512)S(6)} %eq.58, bf16[128,2,32,128]{3,2,1,0:T(8,128)(2,1)} %all-gather.6.cloned.1.call-done), kind=kLoop, calls=%fused_computation.58 | loop fusion | flops 2097152 | bytes 10485761 | tf_op jit(solution)/shard_map/jit(_where)/select_n | solution.py:89
  248.4 1.8 dynamic_update_slice.86
  250.1 5.0 %dynamic_update_slice.88 = bf16[512,2,32,128]{3,0,1,2:T(8,128)(2,1)} pad(bf16[128,2,32,128]{3,0,1,2:T(8,128)(2,1)S(1)} %copy.41, bf16[]{:T(256)} %constant.102.clone.1), padding=0_384x0_0x0_0x0_0 | pad | bytes 10485762 | tf_op jit(solution)/shard_map/dynamic_update_slice | solution.py:102
  255.1 2.2 maximum_maximum_fusion.3
  257.4 2.4 multiply_convert_fusion.10
  259.9 2.6 copy_dynamic-update-slice_fusion.10
  262.5 2.3 multiply_convert_fusion.12
  264.8 1.7 copy_dynamic-update-slice_fusion.11
  266.5 2.3 multiply_convert_fusion.14
  268.8 2.7 copy_dynamic-update-slice_fusion.12
  271.5 14.1 %collective-permute-done.8 = bf16[128,2,32,128]{3,2,1,0:T(8,128)(2,1)} collective-permute-done((bf16[128,2,32,128]{3,2,1,0:T(8,128)(2,1)}, bf16[128,2,32,128]{3,2,1,0:T(8,128)(2,1)}, u32[]{:S(2)}, u32[]{:S(2)}) %collective-permute-start.8) | collective-permute-done | bytes 2097184 | tf_op jit(solution)/shard_map/ppermute | solution.py:23
  285.6 3.2 broadcast_select_fusion.8
  288.8 2.3 multiply_convert_fusion.5
  291.9 4.6 %broadcast_select_fusion.2 = (bf16[128,2,32,128]{3,2,1,0:T(8,128)(2,1)}, bf16[128,2,32,128]{3,2,1,0:T(8,128)(2,1)}) fusion(bf16[128,2,32,128]{3,2,1,0:T(8,128)(2,1)} %collective-permute-done.8, bf16[128,2,32,128]{3,2,1,0:T(8,128)(2,1)} %collective-permute-done.6, pred[]{:T(512)S(6)} %eq.58, bf16[128,2,32,128]{3,2,1,0:T(8,128)(2,1)} %all-gather.8.cloned.1.call-done), kind=kLoop, calls=%fused_computation.56 | loop fusion | flops 2097152 | bytes 10485761 | tf_op jit(solution)/shard_map/jit(_where)/select_n | solution.py:89
  297.1 2.3 multiply_convert_fusion.7
  299.4 2.6 copy_dynamic-update-slice_fusion.5
  303.5 2.7 copy_dynamic-update-slice_fusion.9
  306.2 2.3 multiply_convert_fusion.6
  308.5 3.1 copy_dynamic-update-slice_fusion.6
  311.5 2.3 multiply_convert_fusion.8
  315.3 19.3 %collective-permute-done.12 = bf16[128,2,32,128]{3,2,1,0:T(8,128)(2,1)S(1)} collective-permute-done((bf16[128,2,32,128]{3,2,1,0:T(8,128)(2,1)}, bf16[128,2,32,128]{3,2,1,0:T(8,128)(2,1)S(1)}, u32[]{:S(2)}, u32[]{:S(2)}) %collective-permute-start.12) | collective-permute-done | bytes 2097184 | tf_op jit(solution)/shard_map/ppermute | solution.py:23
  334.6 1.9 broadcast_select_fusion
  339.3 3.9 multiply_convert_fusion.2
  343.2 2.6 copy_dynamic-update-slice_fusion.2
  345.9 2.3 multiply_convert_fusion.4
  351.2 2.8 copy_dynamic-update-slice_fusion
  355.5 3.2 copy-done.8
  358.7 2.6 broadcast_in_dim.21
  361.4 6.4 %bitcast_dynamic-update-slice_fusion.4 = bf16[1,5,32,256,128]{4,3,2,1,0:T(8,128)(2,1)S(1)} fusion(bf16[1,5,32,256,128]{4,3,2,1,0:T(8,128)(2,1)S(1)} %broadcast_in_dim.21, s32[]{:T(128)S(6)} %select_n.155, f32[]{:T(128)S(6)} %select_n.154, bf16[512,2,32,128]{3,0,1,2:T(8,128)(2,1)} %copy_dynamic-update-slice_fusion.9, ...), kind=kOutput, calls=%fused_computation.38 | convolution fusion | flops 2150629376 | bytes 11010056 | tf_op jit(solution)/shard_map/lK,Kst->lst/dot_general | solution.py:119
  367.8 2.8 bitcast_dynamic-update-slice_fusion.3
  370.6 2.8 bitcast_dynamic-update-slice_fusion.2
  373.5 2.8 bitcast_dynamic-update-slice_fusion.1
  376.4 4.1 %copy-done.6 = bf16[1,5,32,256,128]{4,3,2,1,0:T(8,128)(2,1)} copy-done((bf16[1,5,32,256,128]{4,3,2,1,0:T(8,128)(2,1)}, bf16[1,5,32,256,128]{4,3,2,1,0:T(8,128)(2,1)S(1)}, u32[]{:S(2)}) %copy-start.6) | copy-done | bytes 10485784
  380.4 7.0 %bitcast_dynamic-update-slice_fusion = bf16[1,5,32,256,128]{4,3,2,1,0:T(8,128)(2,1)} fusion(bf16[1,5,32,256,128]{4,3,2,1,0:T(8,128)(2,1)} %copy-done.6, s32[]{:T(128)S(6)} %select_n.163, f32[]{:T(128)S(6)} %select_n.162, bf16[512,2,32,128]{3,0,1,2:T(8,128)(2,1)} %copy_dynamic-update-slice_fusion.5, bf16[256,512,1]{1,0,2:T(8,128)(2,1)S(1)} %copy-done.10, ...), kind=kOutput, calls=%fused_computation.34 | convolution fusion | flops 2150629376 | bytes 11010056 | tf_op jit(solution)/shard_map/lK,Kst->lst/dot_general | solution.py:119
  (104 shorter events, 40.2 us)
Async XLA Ops:
  6.5 51.1 %all-gather.12.cloned.1.call-start = ((), (), s32[]{:S(2)}) async-start(), calls=%async_computation.3 | async-start | bytes 2621440 | tf_op jit(solution)/shard_map/all_gather | solution.py:72
  8.4 97.0 %all-gather.6.cloned.1.call-start = ((), (), s32[]{:S(2)}) async-start(), calls=%async_computation | async-start | bytes 2621440 | tf_op jit(solution)/shard_map/all_gather | solution.py:72
  57.6 100.7 %all-gather.8.cloned.1.call-start = ((), (), s32[]{:S(2)}) async-start(), calls=%async_computation.1 | async-start | bytes 2621440 | tf_op jit(solution)/shard_map/all_gather | solution.py:72
  57.7 47.8 %collective-permute-start = (bf16[128,2,32,128]{3,2,1,0:T(8,128)(2,1)}, bf16[128,2,32,128]{3,2,1,0:T(8,128)(2,1)}, u32[]{:S(2)}, u32[]{:S(2)}) collective-permute-start(bf16[128,2,32,128]{3,2,1,0:T(8,128)(2,1)} %bitcast.179), channel_id=1, source_target_pairs={{0,4},{1,5},{2,6},{3,7},{4,0},{5,1},{6,2},{7,3},{8,12},{9,13},{10,... | collective-permute-start | bytes 6291464 | tf_op jit(solution)/shard_map/ppermute | solution.py:23
  62.9 42.8 %copy-start.12 = (s32[1,5]{1,0:T(1,128)S(1)}, s32[1,5]{1,0:T(1,128)}, u32[]{:S(2)}) copy-start(s32[1,5]{1,0:T(1,128)} %param.5) | copy-start | bytes 64
  105.4 116.9 %all-gather.10.cloned.1.call-start = ((), (), s32[]{:S(2)}) async-start(), calls=%async_computation.2 | async-start | bytes 2621440 | tf_op jit(solution)/shard_map/all_gather | solution.py:72
  107.1 7.5 %copy-start.11 = (s32[512]{0:T(512)S(1)}, s32[512]{0:T(512)}, u32[]{:S(2)}) copy-start(s32[512]{0:T(512)} %constant.138) | copy-start | bytes 6148
  110.3 46.8 %collective-permute-start.1 = (bf16[128,2,32,128]{3,2,1,0:T(8,128)(2,1)}, bf16[128,2,32,128]{3,2,1,0:T(8,128)(2,1)}, u32[]{:S(2)}, u32[]{:S(2)}) collective-permute-start(bf16[128,2,32,128]{3,2,1,0:T(8,128)(2,1)} %broadcast_select_fusion.11), channel_id=1, source_target_pairs={{0,2},{1,3},{2,0},{3,1},{4,6},{5,7},{6,4},{7,5},{8,10},{9,11},{10,... | collective-permute-start | bytes 6291464 | tf_op jit(solution)/shard_map/ppermute | solution.py:23
  111.8 46.5 %collective-permute-start.2 = (bf16[128,2,32,128]{3,2,1,0:T(8,128)(2,1)}, bf16[128,2,32,128]{3,2,1,0:T(8,128)(2,1)}, u32[]{:S(2)}, u32[]{:S(2)}) collective-permute-start(bf16[128,2,32,128]{3,2,1,0:T(8,128)(2,1)} %all-gather.6.cloned.1.call-done), channel_id=1, source_target_pairs={{0,4},{1,5},{2,6},{3,7},{4,0},{5,1},{6,2},{7,3},{8,12},{9,13},{10,... | collective-permute-start | bytes 6291464 | tf_op jit(solution)/shard_map/ppermute | solution.py:23
  125.6 1.6 copy-start.3
  172.8 5.3 %copy-start.4 = (bf16[1,128,2,32,128]{4,3,2,0,1:T(8,128)(2,1)S(1)}, bf16[1,128,2,32,128]{4,3,2,0,1:T(8,128)(2,1)}, u32[]{:S(2)}) copy-start(bf16[1,128,2,32,128]{4,3,2,0,1:T(8,128)(2,1)} %all-gather.12.cloned.1.call-done) | copy-start | bytes 6291460
  176.1 45.6 %collective-permute-start.4 = (bf16[128,2,32,128]{3,2,1,0:T(8,128)(2,1)}, bf16[128,2,32,128]{3,2,1,0:T(8,128)(2,1)}, u32[]{:S(2)}, u32[]{:S(2)}) collective-permute-start(bf16[128,2,32,128]{3,2,1,0:T(8,128)(2,1)} %broadcast_select_fusion.10), channel_id=1, source_target_pairs={{0,2},{1,3},{2,0},{3,1},{4,6},{5,7},{6,4},{7,5},{8,10},{9,11},{10,... | collective-permute-start | bytes 6291464 | tf_op jit(solution)/shard_map/ppermute | solution.py:23
  176.6 45.7 %collective-permute-start.6 = (bf16[128,2,32,128]{3,2,1,0:T(8,128)(2,1)}, bf16[128,2,32,128]{3,2,1,0:T(8,128)(2,1)}, u32[]{:S(2)}, u32[]{:S(2)}) collective-permute-start(bf16[128,2,32,128]{3,2,1,0:T(8,128)(2,1)} %all-gather.8.cloned.1.call-done), channel_id=1, source_target_pairs={{0,4},{1,5},{2,6},{3,7},{4,0},{5,1},{6,2},{7,3},{8,12},{9,13},{10,... | collective-permute-start | bytes 6291464 | tf_op jit(solution)/shard_map/ppermute | solution.py:23
  182.9 39.5 %collective-permute-start.5 = (bf16[128,2,32,128]{3,2,1,0:T(8,128)(2,1)}, bf16[128,2,32,128]{3,2,1,0:T(8,128)(2,1)}, u32[]{:S(2)}, u32[]{:S(2)}) collective-permute-start(bf16[128,2,32,128]{3,2,1,0:T(8,128)(2,1)} %get-tuple-element.186), channel_id=1, source_target_pairs={{0,1},{1,0},{2,3},{3,2},{4,5},{5,4},{6,7},{7,6},{8,9},{9,8},{10,11... | collective-permute-start | bytes 6291464 | tf_op jit(solution)/shard_map/ppermute | solution.py:23
  182.9 39.5 %collective-permute-start.3 = (bf16[128,2,32,128]{3,2,1,0:T(8,128)(2,1)}, bf16[128,2,32,128]{3,2,1,0:T(8,128)(2,1)}, u32[]{:S(2)}, u32[]{:S(2)}) collective-permute-start(bf16[128,2,32,128]{3,2,1,0:T(8,128)(2,1)} %get-tuple-element.187), channel_id=1, source_target_pairs={{0,1},{1,0},{2,3},{3,2},{4,5},{5,4},{6,7},{7,6},{8,9},{9,8},{10,11... | collective-permute-start | bytes 6291464 | tf_op jit(solution)/shard_map/ppermute | solution.py:23
  198.3 2.2 copy-start
  222.4 63.2 %collective-permute-start.10 = (bf16[128,2,32,128]{3,2,1,0:T(8,128)(2,1)}, bf16[128,2,32,128]{3,2,1,0:T(8,128)(2,1)}, u32[]{:S(2)}, u32[]{:S(2)}) collective-permute-start(bf16[128,2,32,128]{3,2,1,0:T(8,128)(2,1)} %all-gather.10.cloned.1.call-done), channel_id=1, source_target_pairs={{0,4},{1,5},{2,6},{3,7},{4,0},{5,1},{6,2},{7,3},{8,12},{9,13},{10,... | collective-permute-start | bytes 6291464 | tf_op jit(solution)/shard_map/ppermute | solution.py:23
  241.9 43.7 %collective-permute-start.8 = (bf16[128,2,32,128]{3,2,1,0:T(8,128)(2,1)}, bf16[128,2,32,128]{3,2,1,0:T(8,128)(2,1)}, u32[]{:S(2)}, u32[]{:S(2)}) collective-permute-start(bf16[128,2,32,128]{3,2,1,0:T(8,128)(2,1)} %broadcast_select_fusion.9), channel_id=1, source_target_pairs={{0,2},{1,3},{2,0},{3,1},{4,6},{5,7},{6,4},{7,5},{8,10},{9,11},{10,... | collective-permute-start | bytes 6291464 | tf_op jit(solution)/shard_map/ppermute | solution.py:23
  247.8 37.7 %collective-permute-start.9 = (bf16[128,2,32,128]{3,2,1,0:T(8,128)(2,1)}, bf16[128,2,32,128]{3,2,1,0:T(8,128)(2,1)}, u32[]{:S(2)}, u32[]{:S(2)}) collective-permute-start(bf16[128,2,32,128]{3,2,1,0:T(8,128)(2,1)} %get-tuple-element.184), channel_id=1, source_target_pairs={{0,1},{1,0},{2,3},{3,2},{4,5},{5,4},{6,7},{7,6},{8,9},{9,8},{10,11... | collective-permute-start | bytes 6291464 | tf_op jit(solution)/shard_map/ppermute | solution.py:23
  247.8 37.7 %collective-permute-start.7 = (bf16[128,2,32,128]{3,2,1,0:T(8,128)(2,1)}, bf16[128,2,32,128]{3,2,1,0:T(8,128)(2,1)}, u32[]{:S(2)}, u32[]{:S(2)}) collective-permute-start(bf16[128,2,32,128]{3,2,1,0:T(8,128)(2,1)} %get-tuple-element.185), channel_id=1, source_target_pairs={{0,1},{1,0},{2,3},{3,2},{4,5},{5,4},{6,7},{7,6},{8,9},{9,8},{10,11... | collective-permute-start | bytes 6291464 | tf_op jit(solution)/shard_map/ppermute | solution.py:23
  250.1 14.7 %slice-start = ((s8[8388608]{0:T(1024)(128)(4,1)}), s8[4194304]{0:T(1024)(128)(4,1)S(1)}, s32[]{:S(2)}) async-start(s8[8388608]{0:T(1024)(128)(4,1)} %bitcast.212), calls=%async_computation.4 | async-start | bytes 8388608
  255.1 2.3 copy-start.2
  257.4 7.4 %slice-start.1 = ((s8[8388608]{0:T(1024)(128)(4,1)}), s8[4194304]{0:T(1024)(128)(4,1)S(1)}, s32[]{:S(2)}) async-start(s8[8388608]{0:T(1024)(128)(4,1)} %bitcast.212), calls=%async_computation.5 | async-start | bytes 8388608
  259.9 2.7 copy-start.1
  268.8 16.8 %copy-start.5 = (bf16[128,2,32,128]{3,2,1,0:T(8,128)(2,1)S(1)}, bf16[128,2,32,128]{3,2,1,0:T(8,128)(2,1)}, u32[]{:S(2)}) copy-start(bf16[128,2,32,128]{3,2,1,0:T(8,128)(2,1)} %all-gather.10.cloned.1.call-done) | copy-start | bytes 6291460
  291.8 42.8 %collective-permute-start.12 = (bf16[128,2,32,128]{3,2,1,0:T(8,128)(2,1)}, bf16[128,2,32,128]{3,2,1,0:T(8,128)(2,1)S(1)}, u32[]{:S(2)}, u32[]{:S(2)}) collective-permute-start(bf16[128,2,32,128]{3,2,1,0:T(8,128)(2,1)} %broadcast_select_fusion.8), channel_id=1, source_target_pairs={{0,2},{1,3},{2,0},{3,1},{4,6},{5,7},{6,4},{7,5},{8,10},{9,11},{10,... | collective-permute-start | bytes 6291464 | tf_op jit(solution)/shard_map/ppermute | solution.py:23
  296.6 38.1 %collective-permute-start.13 = (bf16[128,2,32,128]{3,2,1,0:T(8,128)(2,1)}, bf16[128,2,32,128]{3,2,1,0:T(8,128)(2,1)}, u32[]{:S(2)}, u32[]{:S(2)}) collective-permute-start(bf16[128,2,32,128]{3,2,1,0:T(8,128)(2,1)} %get-tuple-element.182), channel_id=1, source_target_pairs={{0,1},{1,0},{2,3},{3,2},{4,5},{5,4},{6,7},{7,6},{8,9},{9,8},{10,11... | collective-permute-start | bytes 6291464 | tf_op jit(solution)/shard_map/ppermute | solution.py:23
  296.6 38.1 %collective-permute-start.11 = (bf16[128,2,32,128]{3,2,1,0:T(8,128)(2,1)}, bf16[128,2,32,128]{3,2,1,0:T(8,128)(2,1)}, u32[]{:S(2)}, u32[]{:S(2)}) collective-permute-start(bf16[128,2,32,128]{3,2,1,0:T(8,128)(2,1)} %get-tuple-element.183), channel_id=1, source_target_pairs={{0,1},{1,0},{2,3},{3,2},{4,5},{5,4},{6,7},{7,6},{8,9},{9,8},{10,11... | collective-permute-start | bytes 6291464 | tf_op jit(solution)/shard_map/ppermute | solution.py:23
  336.6 13.1 %collective-permute-start.15 = (bf16[128,2,32,128]{3,2,1,0:T(8,128)(2,1)S(1)}, bf16[128,2,32,128]{3,2,1,0:T(8,128)(2,1)S(1)}, u32[]{:S(2)}, u32[]{:S(2)}) collective-permute-start(bf16[128,2,32,128]{3,2,1,0:T(8,128)(2,1)S(1)} %get-tuple-element.180), channel_id=1, source_target_pairs={{0,1},{1,0},{2,3},{3,2},{4,5},{5,4},{6,7},{7,6},{8,9},{9,8},{10,11... | collective-permute-start | bytes 6291464 | tf_op jit(solution)/shard_map/ppermute | solution.py:23
  336.6 13.0 %collective-permute-start.14 = (bf16[128,2,32,128]{3,2,1,0:T(8,128)(2,1)S(1)}, bf16[128,2,32,128]{3,2,1,0:T(8,128)(2,1)S(1)}, u32[]{:S(2)}, u32[]{:S(2)}) collective-permute-start(bf16[128,2,32,128]{3,2,1,0:T(8,128)(2,1)S(1)} %get-tuple-element.181), channel_id=1, source_target_pairs={{0,1},{1,0},{2,3},{3,2},{4,5},{5,4},{6,7},{7,6},{8,9},{9,8},{10,11... | collective-permute-start | bytes 6291464 | tf_op jit(solution)/shard_map/ppermute | solution.py:23
  339.3 8.8 %copy-start.7 = (bf16[512,2,32,128]{3,0,1,2:T(8,128)(2,1)}, bf16[512,2,32,128]{3,0,1,2:T(8,128)(2,1)S(1)}, u32[]{:S(2)}) copy-start(bf16[512,2,32,128]{3,0,1,2:T(8,128)(2,1)S(1)} %copy_dynamic-update-slice_fusion.3) | copy-start | bytes 25165828
  355.5 3.2 copy-start.8
  358.7 2.6 copy-start.10
  361.3 6.4 %copy-start.9 = (bf16[512,2,32,128]{3,0,1,2:T(8,128)(2,1)S(1)}, bf16[512,2,32,128]{3,0,1,2:T(8,128)(2,1)}, u32[]{:S(2)}) copy-start(bf16[512,2,32,128]{3,0,1,2:T(8,128)(2,1)} %copy-done.8) | copy-start | bytes 25165828
  361.4 9.2 %slice-start.2 = ((s8[8388608]{0:T(1024)(128)(4,1)}), s8[4194304]{0:T(1024)(128)(4,1)S(1)}, s32[]{:S(2)}) async-start(s8[8388608]{0:T(1024)(128)(4,1)} %bitcast.214), calls=%async_computation.6 | async-start | bytes 8388608
  367.7 2.9 slice-start.3
  367.8 5.7 %slice-start.4 = ((s8[8388608]{0:T(1024)(128)(4,1)}), s8[4194304]{0:T(1024)(128)(4,1)S(1)}, s32[]{:S(2)}) async-start(s8[8388608]{0:T(1024)(128)(4,1)} %bitcast.216), calls=%async_computation.8 | async-start | bytes 8388608
  370.6 2.9 slice-start.5
  376.3 4.1 %copy-start.6 = (bf16[1,5,32,256,128]{4,3,2,1,0:T(8,128)(2,1)}, bf16[1,5,32,256,128]{4,3,2,1,0:T(8,128)(2,1)S(1)}, u32[]{:S(2)}) copy-start(bf16[1,5,32,256,128]{4,3,2,1,0:T(8,128)(2,1)S(1)} %bitcast_dynamic-update-slice_fusion.1) | copy-start | bytes 31457284
Sparse Core Ops, SparseCore 0:
  8.9 48.6 all-gather.11
  59.2 44.6 all-gather.5
  105.6 45.0 all-gather.7
  158.5 43.9 all-gather.9
